TPU v7x, 512 devices: a whole 4x8x8 slice. The times are simulated.
512 devices in a mesh: expert: 64 (over z, y), tensor: 8 (over x, core).
Axes of the slice: x: 4, y: 8, z: 8, core: 2. Of those that a mesh axis runs over, the one named last changes fastest.
Arguments:
- hidden_rows: bfloat16 [2, 1024, 3584], P(None, 'expert', 'tensor'), may hold values from -6 to 6
- draft_len: int32 [2, 256], P(None, 'expert'), may hold values from 1 to 4, 640 in all within a row
- expert_ids: int32 [2, 1024, 8], P(None, 'expert'), may hold values from 0 to 55, all different within a row; in each aligned block of 16 rows (0 to 15, 16 to 31, ..., all dimensions but the last counted through in order) at most 4 rows name the same one
- replica: int32 [2, 1024, 8], P(None, 'expert'), may hold values from 0 to 1
- route_gain: float32 [2, 1024, 8], P(None, 'expert'), may hold values from 0.03 to 0.5
- slot_up: bfloat16 [64, 3584, 1024], P('expert', None, 'tensor'), may hold values from -0.09375 to 0.09375
- slot_down: bfloat16 [64, 1024, 3584], P('expert', 'tensor'), may hold values from -0.1875 to 0.1875
- shared_up: bfloat16 [3584, 1024], P(None, 'tensor'), may hold values from -0.09375 to 0.09375
- shared_down: bfloat16 [1024, 3584], P('tensor'), may hold values from -0.1875 to 0.1875
Outputs:
- mixed: bfloat16 [2, 1024, 3584], P(None, 'expert', 'tensor')
Inputs may be any that keep to these rules, and one draw needn't show every extreme that they name: `expert_ids`: in each step, the 16 row places of one index of expert (live or not) name any one expert at most 4 times. Only the first 8 experts have a replica slot; for the other experts the value has no effect. `draft_len`: in each step the lengths of all 256 requests sum to 640.
All inputs are finite; a program needn't handle non-finite values. No bound on the sum of `draft_len` on one device may be relied on, other than what follows from the above.
Results may differ from a plain program's by a relative error of at most 0.019.
Values may be sent and summed in bfloat16 or wider, within the bound.
No kernel may reach another device: no remote copies, remote signals or barrier semaphores. Data moves between devices by JAX's collectives and lax.ppermute only.
A program may use at most 192 MiB of HBM per device.

v0:
```python
import jax
import jax.numpy as jnp
from jax import lax
from jax.sharding import PartitionSpec as P


def route_plan(lengths, chosen, second, gains, slot_count, capacity):
    row_count, top_count = chosen.shape
    span_rows = row_count // lengths.shape[0]
    positions = jnp.arange(row_count, dtype=jnp.int32)
    limit = jnp.repeat(lengths, span_rows, total_repeat_length=row_count)
    live_mask = positions % span_rows < limit
    replicas = slot_count // 8
    experts_all = slot_count - replicas
    slot_index = jnp.where(
        (chosen < replicas) & (second == 1), chosen + experts_all, chosen
    ).reshape(-1)
    valid = jnp.broadcast_to(live_mask[:, None], chosen.shape).reshape(-1)
    onehot = (
        (slot_index[:, None] == jnp.arange(slot_count, dtype=jnp.int32)[None, :]) & valid[:, None]
    ).astype(jnp.int32)
    earlier = jnp.cumsum(onehot, axis=0) - onehot
    order_rank = jnp.sum(earlier * onehot, axis=1)
    target = jnp.where(valid, slot_index * capacity + order_rank, -1)
    buffer_ids = jnp.arange(slot_count * capacity, dtype=jnp.int32)
    picker = jnp.any(
        target.reshape(row_count, top_count)[None, :, :] == buffer_ids[:, None, None], axis=2
    ).astype(jnp.bfloat16)
    weights = (gains * live_mask[:, None].astype(jnp.float32)).reshape(-1)
    return (live_mask, target, picker, weights)


def shards(
    hidden_rows,
    draft_len,
    expert_ids,
    replica,
    route_gain,
    slot_up,
    slot_down,
    shared_up,
    shared_down,
):
    slot_count = lax.axis_size("expert")
    step_count, row_count, _ = hidden_rows.shape
    top_count = expert_ids.shape[2]
    capacity = row_count * top_count // (slot_count - slot_count // 8) + 2
    gathered = lax.all_gather(hidden_rows, "tensor", axis=2, tiled=True)
    width_full = gathered.shape[2]
    plans = [
        route_plan(
            draft_len[index],
            expert_ids[index],
            replica[index],
            route_gain[index],
            slot_count,
            capacity,
        )
        for index in range(step_count)
    ]
    outgoing = []
    for index in range(step_count):
        source = gathered[index]
        packed = jnp.dot(plans[index][2], source, preferred_element_type=jnp.float32).astype(
            jnp.bfloat16
        )
        outgoing.append(packed.reshape(slot_count, capacity, source.shape[1]))
    groups = [[index] for index in range(step_count)]
    returned = [None] * step_count
    for step_group in groups:
        batch = jnp.concatenate([outgoing[index] for index in step_group], axis=1)
        received = lax.all_to_all(batch, "expert", split_axis=0, concat_axis=0, tiled=True)
        flat_rows = received.reshape(-1, width_full)
        hidden = jax.nn.silu(
            jnp.dot(flat_rows, slot_up[0], preferred_element_type=jnp.float32)
        ).astype(jnp.bfloat16)
        partial_value = jnp.dot(hidden, slot_down[0], preferred_element_type=jnp.float32).astype(
            jnp.bfloat16
        )
        partial_value = partial_value.reshape(received.shape[0], -1, width_full)
        answer = lax.all_to_all(partial_value, "expert", split_axis=0, concat_axis=0, tiled=True)
        out_width = answer.shape[2]
        for place, index in enumerate(step_group):
            returned[index] = answer.reshape(-1, out_width)
    routed_terms = []
    shared_terms = []
    for index in range(step_count):
        live_mask, target, picker, weights = plans[index]
        fetched = jnp.take(returned[index], jnp.maximum(target, 0), axis=0).astype(jnp.float32)
        routed = jnp.sum(
            (fetched * weights[:, None]).reshape(row_count, top_count, fetched.shape[1]), axis=1
        )
        shared_act = jax.nn.silu(
            jnp.dot(gathered[index], shared_up, preferred_element_type=jnp.float32)
        ).astype(jnp.bfloat16)
        shared_out = jnp.dot(shared_act, shared_down, preferred_element_type=jnp.float32)
        routed_terms.append(routed)
        shared_terms.append(shared_out)
    live_all = jnp.stack([plans[index][0] for index in range(step_count)]).astype(jnp.float32)[
        :, :, None
    ]
    terms = (jnp.stack(routed_terms) + jnp.stack(shared_terms)) * live_all
    summed = lax.psum_scatter(terms.astype(jnp.bfloat16), "tensor", scatter_dimension=2, tiled=True)
    return summed


def solution(mesh):
    return jax.shard_map(
        shards,
        mesh=mesh,
        in_specs=(
            P(None, "expert", "tensor"),
            P(None, "expert"),
            P(None, "expert", None),
            P(None, "expert", None),
            P(None, "expert", None),
            P("expert", None, "tensor"),
            P("expert", "tensor", None),
            P(None, "tensor"),
            P("tensor", None),
        ),
        out_specs=P(None, "expert", "tensor"),
        check_vma=False,
    )
```

profile of v0, /device:TPU:6, one launch (start us, length us, event | category | flops | bytes accessed | tf_op | source)
XLA Modules:
  0.0 311.1 jit_solution(14471994504677403090)
XLA Ops:
  6.5 0.8 slice_bitcast_fusion.1
  7.3 0.7 pad_clamp_fusion.2
  8.0 0.7 gather_fusion.2
  8.6 0.7 gather_fusion
  9.4 0.1 and.64
  9.5 0.7 fusion.61
  10.3 0.1 squeeze.37
  10.4 0.7 fusion.60
  11.2 0.1 eq.84
  11.3 0.1 fusion.27
  11.4 0.2 reduce_window_sum.31
  11.6 0.2 select_reduce_fusion.1
  11.8 0.1 fusion.33
  11.9 0.1 fusion.16
  12.0 0.9 copy.58
  13.0 18.7 %all_gather.3 = bf16[2,16,3584]{1,0,2:T(2,128)(2,1)S(1)} all-gather(bf16[2,16,448]{1,0,2:T(2,128)(2,1)S(1)} %copy.58), channel_id=1, replica_groups=mesh['expert'=64,'tensor'=8] {'tensor'}, dimensions={2}, use_global_device_ids=true | all-gather | bytes 258048 | tf_op jit(solution)/shard_map/all_gather | solution.py:48
  31.6 3.5 %fusion.58 = (bf16[1,16,3584]{1,0,2:T(2,128)(2,1)S(1)}, bf16[1,16,3584]{1,0,2:T(2,128)(2,1)}) fusion(bf16[2,16,3584]{1,0,2:T(2,128)(2,1)S(1)} %all_gather.3), kind=kLoop, calls=%fused_computation.82 | loop fusion | bytes 458752 | tf_op jit(solution)/shard_map/slice | solution.py:63
  35.1 1.8 copy.73
  36.9 0.7 convolution_convert_fusion.3
  37.5 1.5 reshape.191
  39.0 13.3 %all-to-all-start = ((bf16[64,4,3584]{2,1,0:T(4,128)(2,1)}), bf16[64,4,3584]{2,1,0:T(4,128)(2,1)S(1)}, u32[]{:S(2)}, u32[]{:S(2)}) async-start(bf16[64,4,3584]{2,1,0:T(4,128)(2,1)} %reshape.191), calls=%async_computation | async-start | bytes 3670016 | tf_op jit(solution)/shard_map/all_to_all | solution.py:72
  52.4 0.1 and.69
  52.6 0.1 squeeze.43
  52.8 0.1 eq.93
  52.9 0.1 fusion.29
  53.0 0.2 reduce_window_sum.32
  53.2 0.2 select_reduce_fusion
  53.4 0.1 reduce_sum.44
  53.4 3.5 %copy.76 = bf16[1,16,3584]{2,1,0:T(8,128)(2,1)S(1)} copy(bf16[1,16,3584]{1,0,2:T(2,128)(2,1)} %get-tuple-element.32) | data formatting | bytes 229376
  57.1 0.1 fusion.17
  57.2 1.9 convolution_convert_fusion.2
  59.1 4.1 %reshape.196 = bf16[64,4,3584]{2,1,0:T(4,128)(2,1)} reshape(bf16[256,3584]{1,0:T(8,128)(2,1)} %convolution_convert_fusion.2) | data formatting | bytes 3670016 | tf_op jit(solution)/shard_map/reshape | solution.py:67
  63.2 36.6 %all-to-all-done = bf16[64,4,3584]{2,1,0:T(4,128)(2,1)S(1)} async-done(((bf16[64,4,3584]{2,1,0:T(4,128)(2,1)}), bf16[64,4,3584]{2,1,0:T(4,128)(2,1)S(1)}, u32[]{:S(2)}, u32[]{:S(2)}) %all-to-all-start) | async-done | bytes 1835040 | tf_op jit(solution)/shard_map/all_to_all | solution.py:72
  99.8 8.3 %all-to-all-start.2 = ((bf16[64,4,3584]{2,1,0:T(4,128)(2,1)}), bf16[64,4,3584]{2,1,0:T(4,128)(2,1)}, u32[]{:S(2)}, u32[]{:S(2)}) async-start(bf16[64,4,3584]{2,1,0:T(4,128)(2,1)} %reshape.196), calls=%async_computation.2 | async-start | bytes 3670016 | tf_op jit(solution)/shard_map/all_to_all | solution.py:72
  108.1 1.5 reshape.192
  109.5 2.9 convolution_convert_fusion.1
  112.5 1.5 reshape.193
  114.0 40.7 %all-to-all-done.2 = bf16[64,4,3584]{2,1,0:T(4,128)(2,1)} async-done(((bf16[64,4,3584]{2,1,0:T(4,128)(2,1)}), bf16[64,4,3584]{2,1,0:T(4,128)(2,1)}, u32[]{:S(2)}, u32[]{:S(2)}) %all-to-all-start.2) | async-done | bytes 1835040 | tf_op jit(solution)/shard_map/all_to_all | solution.py:72
  154.6 7.1 %all-to-all-start.1 = ((bf16[64,4,3584]{2,1,0:T(4,128)(2,1)}), bf16[64,4,3584]{2,1,0:T(4,128)(2,1)S(1)}, u32[]{:S(2)}, u32[]{:S(2)}) async-start(bf16[64,4,3584]{2,1,0:T(4,128)(2,1)} %reshape.193), calls=%async_computation.1 | async-start | bytes 3670016 | tf_op jit(solution)/shard_map/all_to_all | solution.py:81
  161.7 3.9 %reshape.197 = bf16[256,3584]{1,0:T(8,128)(2,1)} reshape(bf16[64,4,3584]{2,1,0:T(4,128)(2,1)} %all-to-all-done.2) | data formatting | bytes 3670016 | tf_op jit(solution)/shard_map/reshape | solution.py:73
  165.6 4.2 %convolution_convert_fusion = bf16[256,3584]{1,0:T(8,128)(2,1)} fusion(bf16[1,128,3584]{2,1,0:T(8,128)(2,1)S(1)} %copy-done, bf16[256,3584]{1,0:T(8,128)(2,1)} %reshape.197, bf16[1,3584,128]{2,1,0:T(8,128)(2,1)} %param.22), kind=kOutput, calls=%fused_computation.4 | convolution fusion | flops 470843392 | bytes 5505024 | tf_op jit(solution)/shard_map/dot_general | solution.py:77
  169.8 4.1 %reshape.198 = bf16[64,4,3584]{2,1,0:T(4,128)(2,1)} reshape(bf16[256,3584]{1,0:T(8,128)(2,1)} %convolution_convert_fusion) | data formatting | bytes 3670016 | tf_op jit(solution)/shard_map/reshape | solution.py:80
  173.9 34.2 %all-to-all-done.1 = bf16[64,4,3584]{2,1,0:T(4,128)(2,1)S(1)} async-done(((bf16[64,4,3584]{2,1,0:T(4,128)(2,1)}), bf16[64,4,3584]{2,1,0:T(4,128)(2,1)S(1)}, u32[]{:S(2)}, u32[]{:S(2)}) %all-to-all-start.1) | async-done | bytes 1835040 | tf_op jit(solution)/shard_map/all_to_all | solution.py:81
  208.1 1.3 copy-done.1
  209.4 6.9 %all-to-all-start.3 = ((bf16[64,4,3584]{2,1,0:T(4,128)(2,1)}), bf16[64,4,3584]{2,1,0:T(4,128)(2,1)}, u32[]{:S(2)}, u32[]{:S(2)}) async-start(bf16[64,4,3584]{2,1,0:T(4,128)(2,1)} %reshape.198), calls=%async_computation.3 | async-start | bytes 3670016 | tf_op jit(solution)/shard_map/all_to_all | solution.py:81
  216.5 0.1 mul.89
  216.6 0.1 mul.98
  216.8 0.1 squeeze.41
  217.0 0.1 squeeze.45
  217.2 1.9 convolution_bitcast_fusion
  219.1 0.5 convolution_bitcast_fusion.1
  219.6 3.0 reshape.194
  222.5 2.0 gather_fusion.1
  224.6 36.1 %all-to-all-done.3 = bf16[64,4,3584]{2,1,0:T(4,128)(2,1)} async-done(((bf16[64,4,3584]{2,1,0:T(4,128)(2,1)}), bf16[64,4,3584]{2,1,0:T(4,128)(2,1)}, u32[]{:S(2)}, u32[]{:S(2)}) %all-to-all-start.3) | async-done | bytes 1835040 | tf_op jit(solution)/shard_map/all_to_all | solution.py:81
  260.6 2.9 reshape.199
  263.6 2.0 gather_fusion.3
  265.6 1.9 bitcast_reduce_fusion.1
  267.5 1.9 bitcast_reduce_fusion
  269.5 0.1 fusion.7
  269.6 2.4 copy.69
  272.0 1.6 reshape.243
  273.7 28.8 %reduce-scatter.4.cloned.1.call-done = bf16[448,32]{1,0:T(8,128)(2,1)} async-done(((bf16[3584,32]{1,0:T(8,128)(2,1)}), bf16[448,32]{1,0:T(8,128)(2,1)}) %reduce-scatter.4.cloned.1.call-update) | async-done | bytes 28688
  302.5 1.0 reshape.244
  303.5 0.7 copy.70
  (36 shorter events, 1.1 us)
Async XLA Ops:
  6.5 103.0 %copy-start = (bf16[1,128,3584]{2,1,0:T(8,128)(2,1)S(1)}, bf16[1,128,3584]{2,1,0:T(8,128)(2,1)}, u32[]{:S(2)}) copy-start(bf16[1,128,3584]{2,1,0:T(8,128)(2,1)} %param.23) | copy-start | bytes 2752516
  39.0 60.7 %all-to-all-start = ((bf16[64,4,3584]{2,1,0:T(4,128)(2,1)}), bf16[64,4,3584]{2,1,0:T(4,128)(2,1)S(1)}, u32[]{:S(2)}, u32[]{:S(2)}) async-start(bf16[64,4,3584]{2,1,0:T(4,128)(2,1)} %reshape.191), calls=%async_computation | async-start | bytes 3670016 | tf_op jit(solution)/shard_map/all_to_all | solution.py:72
  99.8 54.9 %all-to-all-start.2 = ((bf16[64,4,3584]{2,1,0:T(4,128)(2,1)}), bf16[64,4,3584]{2,1,0:T(4,128)(2,1)}, u32[]{:S(2)}, u32[]{:S(2)}) async-start(bf16[64,4,3584]{2,1,0:T(4,128)(2,1)} %reshape.196), calls=%async_computation.2 | async-start | bytes 3670016 | tf_op jit(solution)/shard_map/all_to_all | solution.py:72
  154.6 53.5 %all-to-all-start.1 = ((bf16[64,4,3584]{2,1,0:T(4,128)(2,1)}), bf16[64,4,3584]{2,1,0:T(4,128)(2,1)S(1)}, u32[]{:S(2)}, u32[]{:S(2)}) async-start(bf16[64,4,3584]{2,1,0:T(4,128)(2,1)} %reshape.193), calls=%async_computation.1 | async-start | bytes 3670016 | tf_op jit(solution)/shard_map/all_to_all | solution.py:81
  173.9 42.8 %copy-start.4 = (f32[2,16,8]{1,2,0:T(8,128)S(1)}, f32[2,16,8]{1,2,0:T(8,128)}, u32[]{:S(2)}) copy-start(f32[2,16,8]{1,2,0:T(8,128)} %param.21) | copy-start | bytes 3076
  208.1 1.3 copy-start.1
  209.4 51.2 %all-to-all-start.3 = ((bf16[64,4,3584]{2,1,0:T(4,128)(2,1)}), bf16[64,4,3584]{2,1,0:T(4,128)(2,1)}, u32[]{:S(2)}, u32[]{:S(2)}) async-start(bf16[64,4,3584]{2,1,0:T(4,128)(2,1)} %reshape.198), calls=%async_computation.3 | async-start | bytes 3670016 | tf_op jit(solution)/shard_map/all_to_all | solution.py:81
  216.3 2.8 copy-start.2
  216.3 2.8 copy-start.3
  216.3 86.2 %reduce-scatter.4.cloned.1.call-start = ((), (), s32[]{:S(2)}) async-start(), calls=%async_computation.5 | async-start | bytes 1032192
Sparse Core Ops, SparseCore 0:
  273.8 28.6 reduce-scatter.3
where the time goes:
time: 315 us; the launch traced here: 311 us
  waiting for transfers between devices  176 us (56%)
  local copies, waits for them, and re-layouts  48.6 us (15%)
  starting transfers between devices  35.6 us (11%)
  blocking collectives  18.7 us (6%)
  between operations  13.7 us (4%)
  matrix products  12.1 us (4%)
  other arithmetic  6 us (2%)
    all_to_all x2, waiting for transfers between devices, shards(): lax.all_to_all(batch, 'expert', split_axis=0, concat_axis=0, tiled=True)  77.3 us
    all_to_all x2, waiting for transfers between devices, shards(): lax.all_to_all(partial_value, 'expert', split_axis=0, concat_axis=0, tile...  70.3 us
    unnamed x2, waiting for transfers between devices  28.8 us
    all_to_all x2, starting transfers between devices, shards(): lax.all_to_all(batch, 'expert', split_axis=0, concat_axis=0, tiled=True)  21.6 us
    all_gather x1, blocking collectives, shards(): gathered = lax.all_gather(hidden_rows, 'tensor', axis=2, tiled=True)  18.7 us
    all_to_all x2, starting transfers between devices, shards(): lax.all_to_all(partial_value, 'expert', split_axis=0, concat_axis=0, tile...  14 us
    unnamed x21, local copies, waits for them, and re-layouts  13.6 us
    dot_general x2, matrix products, shards(): jnp.dot(hidden, slot_down[0], preferred_element_type=jnp.float32)  7.1 us
  transfers between devices with their start and end apart: 5, of which 5 were waited for; matrix products, arithmetic and copies ran while one was open for 12% of the time, Pallas kernels for 0%

commit v1 on v0

v1 whole, which is shorter than its diff:
```python
import jax
import jax.numpy as jnp
from jax import lax
from jax.sharding import PartitionSpec as P


def route_plan(lengths, chosen, second, gains, slot_count, capacity):
    row_count, top_count = chosen.shape
    span_rows = row_count // lengths.shape[0]
    positions = jnp.arange(row_count, dtype=jnp.int32)
    limit = jnp.repeat(lengths, span_rows, total_repeat_length=row_count)
    live_mask = positions % span_rows < limit
    replicas = slot_count // 8
    experts_all = slot_count - replicas
    slot_index = jnp.where(
        (chosen < replicas) & (second == 1), chosen + experts_all, chosen
    ).reshape(-1)
    valid = jnp.broadcast_to(live_mask[:, None], chosen.shape).reshape(-1)
    onehot = (
        (slot_index[:, None] == jnp.arange(slot_count, dtype=jnp.int32)[None, :]) & valid[:, None]
    ).astype(jnp.int32)
    earlier = jnp.cumsum(onehot, axis=0) - onehot
    order_rank = jnp.sum(earlier * onehot, axis=1)
    target = jnp.where(valid, slot_index * capacity + order_rank, -1)
    buffer_ids = jnp.arange(slot_count * capacity, dtype=jnp.int32)
    picker = jnp.any(
        target.reshape(row_count, top_count)[None, :, :] == buffer_ids[:, None, None], axis=2
    ).astype(jnp.bfloat16)
    weights = (gains * live_mask[:, None].astype(jnp.float32)).reshape(-1)
    return (live_mask, target, picker, weights)


def shards(
    hidden_rows,
    draft_len,
    expert_ids,
    replica,
    route_gain,
    slot_up,
    slot_down,
    shared_up,
    shared_down,
):
    slot_count = lax.axis_size("expert")
    tensor_count = lax.axis_size("tensor")
    step_count, row_count, width_part = hidden_rows.shape
    top_count = expert_ids.shape[2]
    capacity = row_count * top_count // (slot_count - slot_count // 8) + 2
    plans = [
        route_plan(
            draft_len[index],
            expert_ids[index],
            replica[index],
            route_gain[index],
            slot_count,
            capacity,
        )
        for index in range(step_count)
    ]
    outgoing = []
    for index in range(step_count):
        packed = jnp.dot(
            plans[index][2], hidden_rows[index], preferred_element_type=jnp.float32
        ).astype(jnp.bfloat16)
        outgoing.append(packed.reshape(slot_count, capacity, width_part))
    batch = jnp.concatenate(outgoing, axis=1)
    received = lax.all_to_all(batch, "expert", split_axis=0, concat_axis=0, tiled=True)
    served = received.shape[0] * received.shape[1]
    own = step_count * row_count
    rows_part = jnp.concatenate(
        [received.reshape(served, width_part), hidden_rows.reshape(own, width_part)], axis=0
    )
    rows_all = lax.all_gather(rows_part, "tensor", axis=0, tiled=False)
    up_w = slot_up[0].reshape(tensor_count, width_part, -1)
    shared_w = shared_up.reshape(tensor_count, width_part, -1)
    hidden = jax.nn.silu(
        jnp.einsum("tmc,tch->mh", rows_all[:, :served], up_w, preferred_element_type=jnp.float32)
    ).astype(jnp.bfloat16)
    shared_act = jax.nn.silu(
        jnp.einsum("tmc,tch->mh", rows_all[:, served:], shared_w, preferred_element_type=jnp.float32)
    ).astype(jnp.bfloat16)
    down_w = slot_down[0].reshape(-1, tensor_count, width_part)
    shared_dw = shared_down.reshape(-1, tensor_count, width_part)
    part_value = jnp.einsum(
        "mh,htc->tmc", hidden, down_w, preferred_element_type=jnp.float32
    ).astype(jnp.bfloat16)
    shared_value = jnp.einsum(
        "mh,htc->tmc", shared_act, shared_dw, preferred_element_type=jnp.float32
    ).astype(jnp.bfloat16)
    both = jnp.concatenate([part_value, shared_value], axis=1)
    summed = lax.psum_scatter(both, "tensor", scatter_dimension=0, tiled=True)[0]
    routed_back = summed[:served].reshape(received.shape)
    shared_own = summed[served:].astype(jnp.float32).reshape(step_count, row_count, width_part)
    answer = lax.all_to_all(routed_back, "expert", split_axis=0, concat_axis=0, tiled=True)
    results = []
    for index in range(step_count):
        live_mask, target, picker, weights = plans[index]
        slot_rows = answer[:, index * capacity : (index + 1) * capacity].reshape(-1, width_part)
        fetched = jnp.take(slot_rows, jnp.maximum(target, 0), axis=0).astype(jnp.float32)
        routed = jnp.sum(
            (fetched * weights[:, None]).reshape(row_count, top_count, width_part), axis=1
        )
        live = live_mask.astype(jnp.float32)[:, None]
        results.append(((routed + shared_own[index]) * live).astype(jnp.bfloat16))
    return jnp.stack(results)


def solution(mesh):
    return jax.shard_map(
        shards,
        mesh=mesh,
        in_specs=(
            P(None, "expert", "tensor"),
            P(None, "expert"),
            P(None, "expert", None),
            P(None, "expert", None),
            P(None, "expert", None),
            P("expert", None, "tensor"),
            P("expert", "tensor", None),
            P(None, "tensor"),
            P("tensor", None),
        ),
        out_specs=P(None, "expert", "tensor"),
        check_vma=False,
    )
```

time: 315 us -> 190 us (0.60)
  waiting for transfers between devices: 176 us -> 87.3 us
  local copies, waits for them, and re-layouts: 48.6 us -> 13.8 us
  starting transfers between devices: 35.6 us -> 13.3 us
  blocking collectives: 18.7 us -> 36.1 us
  other arithmetic: 6 us -> 11.2 us
    all_to_all x4 -> x1, waiting for transfers between devices: 148 us -> 18.1 us  [shards(): lax.all_to_all(routed_back, 'expert', split_axis=0, concat_axis=0, tiled=...]
    reduce_scatter x0 -> x1, waiting for transfers between devices: none -> 41.3 us  [shards(): lax.psum_scatter(both, 'tensor', scatter_dimension=0, tiled=True)[0]]
    all_to_all x0 -> x1, blocking collectives: none -> 36.1 us  [shards(): lax.all_to_all(batch, 'expert', split_axis=0, concat_axis=0, tiled=True)]
    unnamed x2, waiting for transfers between devices: 28.8 us -> 0.03 us
    all_gather x0 -> x1, waiting for transfers between devices: none -> 27.8 us  [shards(): rows_all = lax.all_gather(rows_part, 'tensor', axis=0, tiled=False)]
    all_to_all x4 -> x1, starting transfers between devices: 35.6 us -> 13.3 us  [shards(): lax.all_to_all(routed_back, 'expert', split_axis=0, concat_axis=0, tiled=...]
    reshape x8 -> x4, local copies, waits for them, and re-layouts: 22.4 us -> 0.41 us  [the longest x2 0.26 us: shards(): answer[:, index * capacity:(index + 1) * capacity].reshape(-1, width_part)]
    all_gather x1 -> x0, blocking collectives: 18.7 us -> none  [shards(): gathered = lax.all_gather(hidden_rows, 'tensor', axis=2, tiled=True)]
  transfers between devices with their start and end apart: 5 -> 3, of which waited for: 5 -> 3; matrix products, arithmetic and copies ran while one was open for 12% -> 2% of each run, Pallas kernels for 0% -> 0%
where the time goes in v1:
time: 190 us; the launch traced here: 188 us
  waiting for transfers between devices  87.3 us (46%)
  blocking collectives  36.1 us (19%)
  local copies, waits for them, and re-layouts  13.8 us (7%)
  between operations  13.8 us (7%)
  starting transfers between devices  13.3 us (7%)
  matrix products  12.2 us (6%)
  other arithmetic  11.2 us (6%)
    reduce_scatter x1, waiting for transfers between devices, shards(): lax.psum_scatter(both, 'tensor', scatter_dimension=0, tiled=True)[0]  41.3 us
    all_to_all x1, blocking collectives, shards(): lax.all_to_all(batch, 'expert', split_axis=0, concat_axis=0, tiled=True)  36.1 us
    all_gather x1, waiting for transfers between devices, shards(): rows_all = lax.all_gather(rows_part, 'tensor', axis=0, tiled=False)  27.8 us
    all_to_all x1, waiting for transfers between devices, shards(): lax.all_to_all(routed_back, 'expert', split_axis=0, concat_axis=0, tiled=...  18.1 us
    all_to_all x1, starting transfers between devices, shards(): lax.all_to_all(routed_back, 'expert', split_axis=0, concat_axis=0, tiled=...  13.3 us
    dot_general x1, matrix products, shards(): jnp.einsum('mh,htc->tmc', hidden, down_w, preferred_element_type=jnp.floa...  8.25 us
    concatenate x1, other arithmetic, shards(): both = jnp.concatenate([part_value, shared_value], axis=1)  4.63 us
  transfers between devices with their start and end apart: 3, of which 3 were waited for; matrix products, arithmetic and copies ran while one was open for 2% of the time, Pallas kernels for 0%

profile of v1, /device:TPU:6, one launch (start us, length us, event | category | flops | bytes accessed | tf_op | source)
XLA Modules:
  0.0 187.8 jit_solution(15816872353171215600)
XLA Ops:
  6.5 0.8 pad_clamp_fusion.2
  7.3 0.8 slice_bitcast_fusion.3
  8.1 0.7 gather_fusion
  8.7 0.7 gather_fusion.1
  9.4 0.5 fusion.54
  10.0 0.1 and.64
  10.1 0.7 fusion.58
  10.9 0.1 eq.84
  11.0 0.8 fusion.59
  11.9 0.1 squeeze.30
  12.0 0.1 fusion.26
  12.1 0.2 reduce_window_sum.31
  12.3 0.2 select_reduce_fusion.1
  12.5 0.1 reduce_sum.41
  12.5 0.1 fusion.44
  12.6 0.1 fusion.21
  12.7 1.0 convolution_convert_fusion.1
  13.7 0.1 copy.98
  14.0 0.1 and.69
  14.2 0.1 eq.93
  14.4 0.1 squeeze.33
  14.5 0.1 fusion.28
  14.6 0.2 reduce_window_sum.32
  14.8 0.2 select_reduce_fusion
  15.0 0.1 reduce_sum.43
  15.1 0.1 fusion.48
  15.1 0.1 fusion.22
  15.3 0.3 copy-done.6
  15.6 1.0 convolution_convert_fusion
  16.6 0.1 copy.103
  16.8 0.3 pad_maximum_fusion.2
  17.1 36.1 %all_to_all.10 = bf16[64,8,448]{2,1,0:T(8,128)(2,1)S(1)} all-to-all(bf16[64,8,448]{2,1,0:T(8,128)(2,1)S(1)} %pad_maximum_fusion.2), channel_id=1, replica_groups=mesh['expert'=64,'tensor'=8] {'expert'}, dimensions={0} | all-to-all | bytes 917504 | tf_op jit(solution)/shard_map/all_to_all | solution.py:67
  53.2 1.6 pad_maximum_fusion.1
  54.9 1.3 copy.106
  56.2 0.6 copy.108
  56.8 27.8 %all-gather.3.cloned.1.call-done = bf16[4352,448]{1,0:T(8,128)(2,1)} async-done(((bf16[544,448]{1,0:T(8,128)(2,1)}), bf16[4352,448]{1,0:T(8,128)(2,1)}) %all-gather.3.cloned.1.call-update) | async-done | bytes 3899408 | tf_op jit(solution)/shard_map/all_gather | solution.py:73
  84.6 2.0 %fusion.37 = bf16[32,8,448]{2,0,1:T(8,128)(2,1)S(1)} fusion(bf16[128,8,448]{0,2,1:T(8,128)(2,1)S(1)} %bitcast.86, bf16[8,448,128]{2,1,0:T(8,128)(2,1)} %bitcast.89, bf16[8,544,448]{2,1,0:T(8,128)(2,1)} %bitcast.92), kind=kOutput, calls=%fused_computation.50 | convolution fusion | flops 58740736 | bytes 2326528 | tf_op jit(solution)/shard_map/mh,htc->tmc/dot_general | solution.py:87
  86.6 0.2 copy.130
  86.7 0.5 copy.110
  87.2 8.3 %convert_bitcast_fusion = bf16[8,512,448]{1,2,0:T(8,128)(2,1)} fusion(bf16[128,8,448]{0,2,1:T(8,128)(2,1)} %bitcast.90, bf16[8,448,128]{2,1,0:T(8,128)(2,1)S(1)} %bitcast.85, bf16[8,544,448]{2,1,0:T(8,128)(2,1)} %bitcast.93), kind=kOutput, calls=%fused_computation.7 | convolution fusion | flops 941686784 | bytes 9699328 | tf_op jit(solution)/shard_map/mh,htc->tmc/dot_general | solution.py:84
  95.5 4.6 %pad_maximum_fusion = bf16[8,544,448]{1,2,0:T(8,128)(2,1)} fusion(bf16[8,32,448]{1,2,0:T(8,128)(2,1)S(1)} %copy.110, bf16[8,512,448]{1,2,0:T(8,128)(2,1)} %convert_bitcast_fusion), kind=kLoop, calls=%fused_computation.4 | loop fusion | flops 7798784 | bytes 7798784 | tf_op jit(solution)/shard_map/concatenate | solution.py:90
  100.2 0.6 copy-done.9
  100.8 0.1 mul.106
  101.0 0.1 squeeze.36
  101.2 0.1 mul.98
  101.3 0.1 squeeze.35
  101.4 41.3 %reduce-scatter.2.cloned.1.call-done = bf16[1,544,448]{1,2,0:T(8,128)(2,1)} async-done(((bf16[8,544,448]{1,2,0:T(8,128)(2,1)}), bf16[1,544,448]{1,2,0:T(8,128)(2,1)}) %reduce-scatter.2.cloned.1.call-update) | async-done | bytes 487440 | tf_op jit(solution)/shard_map/reduce_scatter | solution.py:91
  142.8 1.0 slice.114
  143.8 1.0 copy.111
  144.8 13.3 %all-to-all-start.1 = ((bf16[64,8,448]{2,1,0:T(8,128)(2,1)}), bf16[64,8,448]{2,1,0:T(8,128)(2,1)S(1)}, u32[]{:S(2)}, u32[]{:S(2)}) async-start(bf16[64,8,448]{2,1,0:T(8,128)(2,1)} %bitcast.19), calls=%async_computation.2 | async-start | bytes 1048576 | tf_op jit(solution)/shard_map/all_to_all | solution.py:94
  158.2 0.9 slice_convert_fusion
  159.1 18.1 %all-to-all-done.1 = bf16[64,8,448]{2,1,0:T(8,128)(2,1)S(1)} async-done(((bf16[64,8,448]{2,1,0:T(8,128)(2,1)}), bf16[64,8,448]{2,1,0:T(8,128)(2,1)S(1)}, u32[]{:S(2)}, u32[]{:S(2)}) %all-to-all-start.1) | async-done | bytes 458784 | tf_op jit(solution)/shard_map/all_to_all | solution.py:94
  177.2 0.2 fusion.56
  177.4 0.1 reshape.219
  177.6 0.8 gather_fusion.3
  178.4 0.2 bitcast_reduce_fusion
  178.6 0.1 copy.115
  178.7 0.1 reshape.217
  178.8 0.8 gather_fusion.2
  179.7 0.2 bitcast_reduce_fusion.1
  179.9 0.1 copy.113
  180.0 0.1 fusion.23
  180.2 0.1 copy.117
  180.3 0.6 pad_maximum_fusion.3
  (46 shorter events, 1.1 us)
Async XLA Ops:
  6.5 80.7 %copy-start = (bf16[1,3584,128]{2,1,0:T(8,128)(2,1)S(1)}, bf16[1,3584,128]{2,1,0:T(8,128)(2,1)}, u32[]{:S(2)}) copy-start(bf16[1,3584,128]{2,1,0:T(8,128)(2,1)} %param.22) | copy-start | bytes 2752516
  6.5 48.3 %copy-start.1 = (bf16[1,128,3584]{2,1,0:T(8,128)(2,1)S(1)}, bf16[1,128,3584]{2,1,0:T(8,128)(2,1)}, u32[]{:S(2)}) copy-start(bf16[1,128,3584]{2,1,0:T(8,128)(2,1)} %param.23) | copy-start | bytes 2752516
  6.5 78.0 %all-gather.3.cloned.1.call-start = ((), (), s32[]{:S(2)}) async-start(), calls=%async_computation.4 | async-start | bytes 5013504 | tf_op jit(solution)/shard_map/all_gather | solution.py:73
  10.8 45.4 %copy-start.2 = (bf16[128,3584]{1,0:T(8,128)(2,1)S(1)}, bf16[128,3584]{1,0:T(8,128)(2,1)}, u32[]{:S(2)}) copy-start(bf16[128,3584]{1,0:T(8,128)(2,1)} %param.25) | copy-start | bytes 2752516
  12.4 1.5 copy-start.4
  15.0 0.6 copy-start.6
  54.8 88.0 %reduce-scatter.2.cloned.1.call-start = ((), (), s32[]{:S(2)}) async-start(), calls=%async_computation.3 | async-start | bytes 5160960 | tf_op jit(solution)/shard_map/reduce_scatter | solution.py:91
  100.1 0.6 copy-start.9
  100.1 0.8 copy-start.3
  100.1 0.9 copy-start.8
  100.1 58.0 %copy-start.7 = (s32[128]{0:T(128)S(1)}, s32[128]{0:T(128)}, u32[]{:S(2)}) copy-start(s32[128]{0:T(128)} %copy-done.6) | copy-start | bytes 1540
  100.1 58.0 %copy-start.5 = (s32[128]{0:T(128)S(1)}, s32[128]{0:T(128)}, u32[]{:S(2)}) copy-start(s32[128]{0:T(128)} %copy-done.4) | copy-start | bytes 1540
  144.8 32.4 %all-to-all-start.1 = ((bf16[64,8,448]{2,1,0:T(8,128)(2,1)}), bf16[64,8,448]{2,1,0:T(8,128)(2,1)S(1)}, u32[]{:S(2)}, u32[]{:S(2)}) async-start(bf16[64,8,448]{2,1,0:T(8,128)(2,1)} %bitcast.19), calls=%async_computation.2 | async-start | bytes 1048576 | tf_op jit(solution)/shard_map/all_to_all | solution.py:94
Sparse Core Ops, SparseCore 0:
  54.9 29.5 all-gather.2
  100.3 42.4 reduce-scatter.1

commit v2 on v1

--- a/solution.py
+++ b/solution.py
@@ -71,23 +71,24 @@
         [received.reshape(served, width_part), hidden_rows.reshape(own, width_part)], axis=0
     )
     rows_all = lax.all_gather(rows_part, "tensor", axis=0, tiled=False)
-    up_w = slot_up[0].reshape(tensor_count, width_part, -1)
-    shared_w = shared_up.reshape(tensor_count, width_part, -1)
-    hidden = jax.nn.silu(
-        jnp.einsum("tmc,tch->mh", rows_all[:, :served], up_w, preferred_element_type=jnp.float32)
+    hidden_units = slot_up.shape[2]
+    up_w = jnp.concatenate([slot_up[0], shared_up], axis=1).reshape(tensor_count, width_part, -1)
+    up_value = jnp.einsum("tmc,tch->mh", rows_all, up_w, preferred_element_type=jnp.float32)
+    act = jax.nn.silu(up_value).astype(jnp.bfloat16)
+    is_routed = (jnp.arange(served + own) < served)[:, None]
+    act_ext = jnp.concatenate(
+        [
+            jnp.where(is_routed, act[:, :hidden_units], jnp.zeros_like(act[:, :hidden_units])),
+            jnp.where(is_routed, jnp.zeros_like(act[:, hidden_units:]), act[:, hidden_units:]),
+        ],
+        axis=1,
+    )
+    down_w = jnp.concatenate([slot_down[0], shared_down], axis=0)
+    down_w = down_w.reshape(-1, tensor_count, width_part).transpose(1, 0, 2)
+    act_b = jnp.broadcast_to(act_ext[None], (tensor_count,) + act_ext.shape)
+    both = jnp.einsum(
+        "tmh,thc->tmc", act_b, down_w, preferred_element_type=jnp.float32
     ).astype(jnp.bfloat16)
-    shared_act = jax.nn.silu(
-        jnp.einsum("tmc,tch->mh", rows_all[:, served:], shared_w, preferred_element_type=jnp.float32)
-    ).astype(jnp.bfloat16)
-    down_w = slot_down[0].reshape(-1, tensor_count, width_part)
-    shared_dw = shared_down.reshape(-1, tensor_count, width_part)
-    part_value = jnp.einsum(
-        "mh,htc->tmc", hidden, down_w, preferred_element_type=jnp.float32
-    ).astype(jnp.bfloat16)
-    shared_value = jnp.einsum(
-        "mh,htc->tmc", shared_act, shared_dw, preferred_element_type=jnp.float32
-    ).astype(jnp.bfloat16)
-    both = jnp.concatenate([part_value, shared_value], axis=1)
     summed = lax.psum_scatter(both, "tensor", scatter_dimension=0, tiled=True)[0]
     routed_back = summed[:served].reshape(received.shape)
     shared_own = summed[served:].astype(jnp.float32).reshape(step_count, row_count, width_part)

time: 190 us -> 179 us (0.942)
  other arithmetic: 11.2 us -> 5.12 us
  matrix products: 12.2 us -> 9.32 us
  local copies, waits for them, and re-layouts: 13.8 us -> 11 us
    concatenate x1, other arithmetic: 4.63 us -> 0.03 us  [shards(): jnp.concatenate([jnp.where(is_routed, act[:, :hidden_units], jnp.zeros_li...]
    dot_general x2, matrix products: 10.3 us -> 7.35 us  [the longest x1 3.97 us: shards(): jnp.einsum('tmc,tch->mh', rows_all, up_w, preferred_element_type=jnp.floa...]
    slice x2 -> x0, local copies, waits for them, and re-layouts: 2.04 us -> none  [shards(): routed_back = summed[:served].reshape(received.shape)]
where the time goes in v2:
time: 179 us; the launch traced here: 177 us
  waiting for transfers between devices  88.3 us (49%)
  blocking collectives  36.1 us (20%)
  between operations  13.7 us (8%)
  starting transfers between devices  13.3 us (7%)
  local copies, waits for them, and re-layouts  11 us (6%)
  matrix products  9.32 us (5%)
  other arithmetic  5.12 us (3%)
    reduce_scatter x1, waiting for transfers between devices, shards(): lax.psum_scatter(both, 'tensor', scatter_dimension=0, tiled=True)[0]  42.3 us
    all_to_all x1, blocking collectives, shards(): lax.all_to_all(batch, 'expert', split_axis=0, concat_axis=0, tiled=True)  36.1 us
    all_gather x1, waiting for transfers between devices, shards(): rows_all = lax.all_gather(rows_part, 'tensor', axis=0, tiled=False)  28.4 us
    all_to_all x1, waiting for transfers between devices, shards(): lax.all_to_all(routed_back, 'expert', split_axis=0, concat_axis=0, tiled=...  17.6 us
    all_to_all x1, starting transfers between devices, shards(): lax.all_to_all(routed_back, 'expert', split_axis=0, concat_axis=0, tiled=...  13.3 us
    dot_general x1, matrix products, shards(): jnp.einsum('tmc,tch->mh', rows_all, up_w, preferred_element_type=jnp.floa...  3.97 us
  transfers between devices with their start and end apart: 3, of which 3 were waited for; matrix products, arithmetic and copies ran while one was open for 2% of the time, Pallas kernels for 0%

profile of v2, /device:TPU:6, one launch (start us, length us, event | category | flops | bytes accessed | tf_op | source)
XLA Modules:
  0.0 176.9 jit_solution(13980674224071935462)
XLA Ops:
  6.5 0.7 fusion.46
  7.3 0.1 copy.54
  7.3 0.1 eq.84
  7.4 0.7 fusion.47
  8.1 0.1 copy.53
  8.2 0.1 squeeze.32
  8.3 0.7 pad_clamp_fusion.2
  9.0 0.8 slice_bitcast_fusion.4
  9.7 0.7 gather_fusion
  10.4 0.1 broadcast_in_dim.65
  10.5 0.1 and.64
  10.6 0.1 fusion.15
  10.7 0.2 reduce_window_sum.31
  10.9 0.2 select_reduce_fusion.1
  11.1 0.1 reduce_sum.41
  11.1 0.1 fusion.33
  11.2 0.1 fusion.12
  11.4 1.0 convolution_convert_fusion.2
  12.3 0.1 copy.41
  12.5 0.1 reshape.217
  12.6 0.1 copy.56
  12.7 0.1 eq.93
  12.8 0.1 copy.55
  12.8 0.1 squeeze.35
  12.9 0.7 gather_fusion.1
  13.6 0.1 broadcast_in_dim.68
  13.7 0.1 and.69
  13.8 0.1 fusion.17
  13.9 0.2 reduce_window_sum.32
  14.1 0.2 select_reduce_fusion
  14.2 0.1 reduce_sum.43
  14.3 0.1 fusion.37
  14.4 0.1 fusion.13
  14.5 1.0 convolution_convert_fusion.1
  15.5 0.1 copy.46
  15.7 0.1 reshape.218
  15.8 0.3 pad_maximum_fusion.1
  16.0 36.1 %all_to_all.10 = bf16[64,8,448]{2,1,0:T(8,128)(2,1)S(1)} all-to-all(bf16[64,8,448]{2,1,0:T(8,128)(2,1)S(1)} %pad_maximum_fusion.1), channel_id=1, replica_groups=mesh['expert'=64,'tensor'=8] {'expert'}, dimensions={0} | all-to-all | bytes 917504 | tf_op jit(solution)/shard_map/all_to_all | solution.py:67
  52.2 0.9 pad_maximum_fusion
  53.1 0.6 copy.47
  53.7 0.6 copy.48
  54.4 28.4 %all-gather.3.cloned.1.call-done = bf16[4352,448]{1,0:T(8,128)(2,1)} async-done(((bf16[544,448]{1,0:T(8,128)(2,1)}), bf16[4352,448]{1,0:T(8,128)(2,1)}) %all-gather.3.cloned.1.call-update) | async-done | bytes 3899408 | tf_op jit(solution)/shard_map/all_gather | solution.py:73
  82.8 4.0 %multiply_convert_fusion = bf16[544,256]{1,0:T(8,128)(2,1)S(1)} fusion(bf16[8,544,448]{2,1,0:T(8,128)(2,1)} %bitcast.65, bf16[8,448,128]{2,1,0:T(8,128)(2,1)} %bitcast.66, bf16[8,448,128]{2,1,0:T(8,128)(2,1)} %bitcast.67), kind=kOutput, calls=%fused_computation.17 | convolution fusion | flops 1002610688 | bytes 6012928 | tf_op jit(solution)/shard_map/tmc,tch->mh/dot_general | solution.py:76
  86.8 0.1 slice_select_fusion.1
  87.0 3.4 %convolution_convert_fusion = bf16[8,544,448]{2,1,0:T(8,128)(2,1)} fusion(bf16[128,8,448]{0,2,1:T(8,128)(2,1)S(1)} %bitcast.63, bf16[128,8,448]{0,2,1:T(8,128)(2,1)S(1)} %bitcast.62, bf16[544,256]{1,0:T(8,128)(2,1)S(1)} %pad_maximum_fusion.2), kind=kOutput, calls=%fused_computation.4 | convolution fusion | flops 1003864064 | bytes 6012928 | tf_op jit(solution)/shard_map/tmh,thc->tmc/dot_general | solution.py:89
  90.4 42.3 %reduce-scatter.2.cloned.1.call-done = bf16[1,544,448]{2,1,0:T(8,128)(2,1)} async-done(((bf16[8,544,448]{2,1,0:T(8,128)(2,1)}), bf16[1,544,448]{2,1,0:T(8,128)(2,1)}) %reduce-scatter.2.cloned.1.call-update) | async-done | bytes 487440 | tf_op jit(solution)/shard_map/reduce_scatter | solution.py:92
  132.6 1.9 %slice_bitcast_fusion = bf16[64,8,448]{2,1,0:T(8,128)(2,1)} fusion(bf16[1,544,448]{2,1,0:T(8,128)(2,1)} %reduce-scatter.2.cloned.1.call-done), kind=kLoop, calls=%fused_computation.18 | loop fusion | bytes 917504 | tf_op jit(solution)/shard_map/reshape | solution.py:93
  134.5 13.3 %all-to-all-start.1 = ((bf16[64,8,448]{2,1,0:T(8,128)(2,1)}), bf16[64,8,448]{2,1,0:T(8,128)(2,1)S(1)}, u32[]{:S(2)}, u32[]{:S(2)}) async-start(bf16[64,8,448]{2,1,0:T(8,128)(2,1)} %slice_bitcast_fusion), calls=%async_computation.2 | async-start | bytes 1048576 | tf_op jit(solution)/shard_map/all_to_all | solution.py:95
  147.9 0.1 mul.101
  148.0 0.1 copy.50
  148.1 0.1 squeeze.38
  148.2 0.1 mul.93
  148.3 0.1 copy.49
  148.4 0.1 squeeze.37
  148.6 0.8 slice_convert_fusion
  149.3 17.6 %all-to-all-done.1 = bf16[64,8,448]{2,1,0:T(8,128)(2,1)S(1)} async-done(((bf16[64,8,448]{2,1,0:T(8,128)(2,1)}), bf16[64,8,448]{2,1,0:T(8,128)(2,1)S(1)}, u32[]{:S(2)}, u32[]{:S(2)}) %all-to-all-start.1) | async-done | bytes 458784 | tf_op jit(solution)/shard_map/all_to_all | solution.py:95
  166.9 0.2 fusion.44
  167.1 0.1 reshape.222
  167.2 0.1 reshape.224
  167.4 0.8 gather_fusion.2
  168.2 0.8 gather_fusion.3
  169.1 0.3 bitcast_reduce_fusion
  169.3 0.1 fusion.24
  169.4 0.6 pad_maximum_fusion.3
  (29 shorter events, 0.4 us)
Async XLA Ops:
  6.5 45.6 %copy-start.2 = (bf16[2,16,448]{2,1,0:T(8,128)(2,1)S(1)}, bf16[2,16,448]{2,1,0:T(8,128)(2,1)}, u32[]{:S(2)}) copy-start(bf16[2,16,448]{2,1,0:T(8,128)(2,1)} %param.17) | copy-start | bytes 86020
  6.5 76.3 %all-gather.3.cloned.1.call-start = ((), (), s32[]{:S(2)}) async-start(), calls=%async_computation.4 | async-start | bytes 5013504 | tf_op jit(solution)/shard_map/all_gather | solution.py:73
  10.9 42.2 %copy-start = (bf16[1,128,3584]{2,1,0:T(8,128)(2,1)S(1)}, bf16[1,128,3584]{2,1,0:T(8,128)(2,1)}, u32[]{:S(2)}) copy-start(bf16[1,128,3584]{2,1,0:T(8,128)(2,1)} %param.23) | copy-start | bytes 2752516
  13.6 40.1 %copy-start.1 = (bf16[128,3584]{1,0:T(8,128)(2,1)S(1)}, bf16[128,3584]{1,0:T(8,128)(2,1)}, u32[]{:S(2)}) copy-start(bf16[128,3584]{1,0:T(8,128)(2,1)} %param.25) | copy-start | bytes 2752516
  53.0 79.6 %reduce-scatter.2.cloned.1.call-start = ((), (), s32[]{:S(2)}) async-start(), calls=%async_computation.3 | async-start | bytes 5013504 | tf_op jit(solution)/shard_map/reduce_scatter | solution.py:92
  90.3 57.5 %copy-start.3 = (f32[2,16,8]{1,2,0:T(8,128)S(1)}, f32[2,16,8]{1,2,0:T(8,128)}, u32[]{:S(2)}) copy-start(f32[2,16,8]{1,2,0:T(8,128)} %param.21) | copy-start | bytes 3076
  134.5 32.4 %all-to-all-start.1 = ((bf16[64,8,448]{2,1,0:T(8,128)(2,1)}), bf16[64,8,448]{2,1,0:T(8,128)(2,1)S(1)}, u32[]{:S(2)}, u32[]{:S(2)}) async-start(bf16[64,8,448]{2,1,0:T(8,128)(2,1)} %slice_bitcast_fusion), calls=%async_computation.2 | async-start | bytes 1048576 | tf_op jit(solution)/shard_map/all_to_all | solution.py:95
Sparse Core Ops, SparseCore 0:
  53.2 29.5 all-gather.2
  90.5 42.1 reduce-scatter.1

commit v3 on v2

--- a/solution.py
+++ b/solution.py
@@ -57,6 +57,10 @@
         )
         for index in range(step_count)
     ]
+    hidden_units = slot_up.shape[2]
+    down_parts = jnp.concatenate([slot_down[0], shared_down], axis=0)
+    down_parts = down_parts.reshape(-1, tensor_count, width_part).transpose(1, 0, 2)
+    down_cols = lax.all_to_all(down_parts, "tensor", split_axis=0, concat_axis=0, tiled=True)
     outgoing = []
     for index in range(step_count):
         packed = jnp.dot(
@@ -71,27 +75,24 @@
         [received.reshape(served, width_part), hidden_rows.reshape(own, width_part)], axis=0
     )
     rows_all = lax.all_gather(rows_part, "tensor", axis=0, tiled=False)
-    hidden_units = slot_up.shape[2]
     up_w = jnp.concatenate([slot_up[0], shared_up], axis=1).reshape(tensor_count, width_part, -1)
     up_value = jnp.einsum("tmc,tch->mh", rows_all, up_w, preferred_element_type=jnp.float32)
     act = jax.nn.silu(up_value).astype(jnp.bfloat16)
     is_routed = (jnp.arange(served + own) < served)[:, None]
-    act_ext = jnp.concatenate(
-        [
-            jnp.where(is_routed, act[:, :hidden_units], jnp.zeros_like(act[:, :hidden_units])),
-            jnp.where(is_routed, jnp.zeros_like(act[:, hidden_units:]), act[:, hidden_units:]),
-        ],
-        axis=1,
-    )
-    down_w = jnp.concatenate([slot_down[0], shared_down], axis=0)
-    down_w = down_w.reshape(-1, tensor_count, width_part).transpose(1, 0, 2)
-    act_b = jnp.broadcast_to(act_ext[None], (tensor_count,) + act_ext.shape)
-    both = jnp.einsum(
-        "tmh,thc->tmc", act_b, down_w, preferred_element_type=jnp.float32
-    ).astype(jnp.bfloat16)
-    summed = lax.psum_scatter(both, "tensor", scatter_dimension=0, tiled=True)[0]
-    routed_back = summed[:served].reshape(received.shape)
-    shared_own = summed[served:].astype(jnp.float32).reshape(step_count, row_count, width_part)
+    act_own = jnp.where(is_routed, act[:, :hidden_units], act[:, hidden_units:])
+    act_all = lax.all_gather(act_own, "tensor", axis=0, tiled=False)
+    routed_back = jnp.einsum(
+        "imu,iuc->mc",
+        act_all[:, :served],
+        down_cols[:, :hidden_units],
+        preferred_element_type=jnp.float32,
+    ).astype(jnp.bfloat16).reshape(received.shape)
+    shared_own = jnp.einsum(
+        "imu,iuc->mc",
+        act_all[:, served:],
+        down_cols[:, hidden_units:],
+        preferred_element_type=jnp.float32,
+    ).reshape(step_count, row_count, width_part)
     answer = lax.all_to_all(routed_back, "expert", split_axis=0, concat_axis=0, tiled=True)
     results = []
     for index in range(step_count):

time: 179 us -> 168 us (0.939)
  waiting for transfers between devices: 88.3 us -> 47.4 us
  blocking collectives: 36.1 us -> 68.2 us
    reduce_scatter x1 -> x0, waiting for transfers between devices: 42.3 us -> none  [shards(): lax.psum_scatter(both, 'tensor', scatter_dimension=0, tiled=True)[0]]
    all_to_all x0 -> x1, blocking collectives: none -> 32 us  [shards(): lax.all_to_all(down_parts, 'tensor', split_axis=0, concat_axis=0, tiled=T...]
    reshape x1 -> x0, local copies, waits for them, and re-layouts: 1.86 us -> none  [shards(): routed_back = summed[:served].reshape(received.shape)]
  transfers between devices with their start and end apart: 3 -> 3, of which waited for: 3 -> 2; matrix products, arithmetic and copies ran while one was open for 2% -> 2% of each run, Pallas kernels for 0% -> 0%
where the time goes in v3:
time: 168 us; the launch traced here: 166 us
  blocking collectives  68.2 us (41%)
  waiting for transfers between devices  47.4 us (28%)
  between operations  13.7 us (8%)
  starting transfers between devices  13.3 us (8%)
  local copies, waits for them, and re-layouts  10.3 us (6%)
  matrix products  7.93 us (5%)
  other arithmetic  5.19 us (3%)
    all_to_all x1, blocking collectives, shards(): lax.all_to_all(batch, 'expert', split_axis=0, concat_axis=0, tiled=True)  36.2 us
    all_to_all x1, blocking collectives, shards(): lax.all_to_all(down_parts, 'tensor', split_axis=0, concat_axis=0, tiled=T...  32 us
    all_gather x1, waiting for transfers between devices, shards(): rows_all = lax.all_gather(rows_part, 'tensor', axis=0, tiled=False)  29.7 us
    all_to_all x1, waiting for transfers between devices, shards(): lax.all_to_all(routed_back, 'expert', split_axis=0, concat_axis=0, tiled=...  17.7 us
    all_to_all x1, starting transfers between devices, shards(): lax.all_to_all(routed_back, 'expert', split_axis=0, concat_axis=0, tiled=...  13.3 us
    dot_general x1, matrix products, shards(): jnp.einsum('tmc,tch->mh', rows_all, up_w, preferred_element_type=jnp.floa...  3.58 us
  transfers between devices with their start and end apart: 3, of which 2 were waited for; matrix products, arithmetic and copies ran while one was open for 2% of the time, Pallas kernels for 0%

profile of v3, /device:TPU:6, one launch (start us, length us, event | category | flops | bytes accessed | tf_op | source)
XLA Modules:
  0.0 166.0 jit_solution(12937655248027100463)
XLA Ops:
  6.5 0.7 fusion.45
  7.3 0.1 copy.58
  7.3 0.1 eq.84
  7.4 0.7 fusion.46
  8.1 0.1 copy.57
  8.2 0.1 squeeze.31
  8.3 0.7 pad_clamp_fusion.2
  9.0 0.8 slice_bitcast_fusion.1
  9.7 0.7 gather_fusion
  10.4 0.1 broadcast_in_dim.54
  10.5 0.1 and.64
  10.6 0.1 fusion.17
  10.7 0.2 reduce_window_sum.31
  10.9 0.2 select_reduce_fusion.1
  11.1 0.1 reduce_sum.41
  11.1 0.1 fusion.33
  11.2 0.1 fusion.13
  11.4 1.0 convolution_convert_fusion.1
  12.3 0.1 copy.44
  12.5 0.1 reshape.210
  12.6 0.1 copy.60
  12.7 0.1 eq.93
  12.7 0.1 copy.59
  12.8 0.1 squeeze.34
  12.9 0.7 gather_fusion.1
  13.6 0.1 broadcast_in_dim.57
  13.7 0.1 and.69
  13.8 0.1 fusion.19
  13.9 0.2 reduce_window_sum.32
  14.1 0.2 select_reduce_fusion
  14.2 0.1 reduce_sum.43
  14.3 0.1 fusion.37
  14.4 0.1 fusion.14
  14.5 0.3 convolution_convert_fusion
  14.8 0.1 copy.49
  15.0 0.1 reshape.211
  15.1 0.3 pad_maximum_fusion.1
  15.4 36.2 %all_to_all.15 = bf16[64,8,448]{2,1,0:T(8,128)(2,1)S(1)} all-to-all(bf16[64,8,448]{2,1,0:T(8,128)(2,1)S(1)} %pad_maximum_fusion.1), channel_id=1, replica_groups=mesh['expert'=64,'tensor'=8] {'expert'}, dimensions={0} | all-to-all | bytes 917504 | tf_op jit(solution)/shard_map/all_to_all | solution.py:71
  51.6 0.9 pad_maximum_fusion
  52.5 29.7 %all-gather.5.cloned.1.call-done = bf16[4352,448]{1,0:T(8,128)(2,1)} async-done(((bf16[544,448]{1,0:T(8,128)(2,1)}), bf16[4352,448]{1,0:T(8,128)(2,1)}) %all-gather.5.cloned.1.call-update) | async-done | bytes 3899408 | tf_op jit(solution)/shard_map/all_gather | solution.py:77
  82.2 3.6 %multiply_convert_fusion = bf16[544,256]{1,0:T(8,128)(2,1)S(1)} fusion(bf16[8,544,448]{2,1,0:T(8,128)(2,1)} %bitcast.50, bf16[8,448,128]{2,1,0:T(8,128)(2,1)S(1)} %bitcast.53, bf16[8,448,128]{2,1,0:T(8,128)(2,1)S(1)} %bitcast.54), kind=kOutput, calls=%fused_computation.19 | convolution fusion | flops 1002610688 | bytes 6012928 | tf_op jit(solution)/shard_map/tmc,tch->mh/dot_general | solution.py:79
  85.8 0.8 slice_select_fusion
  86.7 0.7 copy.50
  87.4 0.7 copy.51
  88.1 0.2 maximum_bitcast_fusion
  88.3 32.0 %all_to_all.16 = bf16[8,256,448]{1,2,0:T(8,128)(2,1)S(1)} all-to-all(bf16[8,256,448]{1,2,0:T(8,128)(2,1)S(1)} %maximum_bitcast_fusion), channel_id=1, replica_groups=mesh['expert'=64,'tensor'=8] {'tensor'}, dimensions={0} | all-to-all | bytes 3670016 | tf_op jit(solution)/shard_map/all_to_all | solution.py:63
  120.3 1.9 %fusion.4 = bf16[512,448]{0,1:T(8,128)(2,1)S(1)} fusion(bf16[8,544,128]{2,1,0:T(8,128)(2,1)} %bitcast.51, bf16[8,256,448]{1,2,0:T(8,128)(2,1)S(1)} %all_to_all.16), kind=kOutput, calls=%fused_computation.10 | convolution fusion | flops 469991424 | bytes 2424832 | tf_op jit(solution)/shard_map/imu,iuc->mc/dot_general | solution.py:84
  122.2 1.0 copy.52
  123.2 13.3 %all-to-all-start.2 = ((bf16[64,8,448]{2,1,0:T(8,128)(2,1)}), bf16[64,8,448]{2,1,0:T(8,128)(2,1)S(1)}, u32[]{:S(2)}, u32[]{:S(2)}) async-start(bf16[64,8,448]{2,1,0:T(8,128)(2,1)} %bitcast.17), calls=%async_computation.2 | async-start | bytes 1048576 | tf_op jit(solution)/shard_map/all_to_all | solution.py:96
  136.6 0.1 mul.101
  136.7 0.1 copy.54
  136.7 0.1 squeeze.37
  136.9 0.1 mul.93
  137.1 0.1 squeeze.36
  137.2 1.2 convolution_bitcast_fusion.1
  138.4 17.7 %all-to-all-done.2 = bf16[64,8,448]{2,1,0:T(8,128)(2,1)S(1)} async-done(((bf16[64,8,448]{2,1,0:T(8,128)(2,1)}), bf16[64,8,448]{2,1,0:T(8,128)(2,1)S(1)}, u32[]{:S(2)}, u32[]{:S(2)}) %all-to-all-start.2) | async-done | bytes 458784 | tf_op jit(solution)/shard_map/all_to_all | solution.py:96
  156.1 0.2 fusion.43
  156.3 0.1 reshape.215
  156.4 0.1 reshape.217
  156.5 0.8 gather_fusion.2
  157.4 0.8 gather_fusion.3
  158.2 0.2 bitcast_reduce_fusion
  158.5 0.1 fusion.24
  158.6 0.6 pad_maximum_fusion.2
  (34 shorter events, 0.4 us)
Async XLA Ops:
  6.5 8.0 %copy-start.2 = (bf16[2,16,448]{2,1,0:T(8,128)(2,1)S(1)}, bf16[2,16,448]{2,1,0:T(8,128)(2,1)}, u32[]{:S(2)}) copy-start(bf16[2,16,448]{2,1,0:T(8,128)(2,1)} %param.17) | copy-start | bytes 86020
  6.5 75.7 %all-gather.5.cloned.1.call-start = ((), (), s32[]{:S(2)}) async-start(), calls=%async_computation.3 | async-start | bytes 5013504 | tf_op jit(solution)/shard_map/all_gather | solution.py:77
  15.0 67.2 %copy-start.4 = (bf16[3584,128]{1,0:T(8,128)(2,1)S(1)}, bf16[3584,128]{1,0:T(8,128)(2,1)}, u32[]{:S(2)}) copy-start(bf16[3584,128]{1,0:T(8,128)(2,1)} %param.24) | copy-start | bytes 2752516
  15.1 67.2 %copy-start.5 = (bf16[1,3584,128]{2,1,0:T(8,128)(2,1)S(1)}, bf16[1,3584,128]{2,1,0:T(8,128)(2,1)}, u32[]{:S(2)}) copy-start(bf16[1,3584,128]{2,1,0:T(8,128)(2,1)} %param.22) | copy-start | bytes 2752516
  52.5 67.8 %all-gather.7.cloned.1.call-start = ((), (), s32[]{:S(2)}) async-start(), calls=%async_computation.4 | async-start | bytes 1253376 | tf_op jit(solution)/shard_map/all_gather | solution.py:83
  82.2 4.4 %copy-start = (bf16[1,128,3584]{2,1,0:T(8,128)(2,1)S(1)}, bf16[1,128,3584]{2,1,0:T(8,128)(2,1)}, u32[]{:S(2)}) copy-start(bf16[1,128,3584]{2,1,0:T(8,128)(2,1)} %param.23) | copy-start | bytes 2752516
  85.8 1.5 copy-start.1
  122.2 14.3 %copy-start.3 = (f32[2,16,8]{1,2,0:T(8,128)S(1)}, f32[2,16,8]{1,2,0:T(8,128)}, u32[]{:S(2)}) copy-start(f32[2,16,8]{1,2,0:T(8,128)} %param.21) | copy-start | bytes 3076
  123.2 32.9 %all-to-all-start.2 = ((bf16[64,8,448]{2,1,0:T(8,128)(2,1)}), bf16[64,8,448]{2,1,0:T(8,128)(2,1)S(1)}, u32[]{:S(2)}, u32[]{:S(2)}) async-start(bf16[64,8,448]{2,1,0:T(8,128)(2,1)} %bitcast.17), calls=%async_computation.2 | async-start | bytes 1048576 | tf_op jit(solution)/shard_map/all_to_all | solution.py:96
Sparse Core Ops, SparseCore 0:
  52.6 29.5 all-gather.4
  86.8 33.4 all-gather.6

commit v4 on v3

--- a/solution.py
+++ b/solution.py
@@ -30,7 +30,7 @@
     return (live_mask, target, picker, weights)
 
 
-def shards(
+def layer(
     hidden_rows,
     draft_len,
     expert_ids,
@@ -96,7 +96,7 @@
     answer = lax.all_to_all(routed_back, "expert", split_axis=0, concat_axis=0, tiled=True)
     results = []
     for index in range(step_count):
-        live_mask, target, picker, weights = plans[index]
+        live_mask, target, _, weights = plans[index]
         slot_rows = answer[:, index * capacity : (index + 1) * capacity].reshape(-1, width_part)
         fetched = jnp.take(slot_rows, jnp.maximum(target, 0), axis=0).astype(jnp.float32)
         routed = jnp.sum(
@@ -109,7 +109,7 @@
 
 def solution(mesh):
     return jax.shard_map(
-        shards,
+        layer,
         mesh=mesh,
         in_specs=(
             P(None, "expert", "tensor"),

time: 168 us -> 168 us (level)
  no operation moved by 1% of the time
where the time goes in v4:
time: 168 us; the launch traced here: 166 us
  blocking collectives  68.2 us (41%)
  waiting for transfers between devices  47.4 us (28%)
  between operations  13.7 us (8%)
  starting transfers between devices  13.3 us (8%)
  local copies, waits for them, and re-layouts  10.3 us (6%)
  matrix products  7.93 us (5%)
  other arithmetic  5.19 us (3%)
    all_to_all x1, blocking collectives, layer(): lax.all_to_all(batch, 'expert', split_axis=0, concat_axis=0, tiled=True)  36.2 us
    all_to_all x1, blocking collectives, layer(): lax.all_to_all(down_parts, 'tensor', split_axis=0, concat_axis=0, tiled=T...  32 us
    all_gather x1, waiting for transfers between devices, layer(): rows_all = lax.all_gather(rows_part, 'tensor', axis=0, tiled=False)  29.7 us
    all_to_all x1, waiting for transfers between devices, layer(): lax.all_to_all(routed_back, 'expert', split_axis=0, concat_axis=0, tiled=...  17.7 us
    all_to_all x1, starting transfers between devices, layer(): lax.all_to_all(routed_back, 'expert', split_axis=0, concat_axis=0, tiled=...  13.3 us
    dot_general x1, matrix products, layer(): jnp.einsum('tmc,tch->mh', rows_all, up_w, preferred_element_type=jnp.floa...  3.58 us
  transfers between devices with their start and end apart: 3, of which 2 were waited for; matrix products, arithmetic and copies ran while one was open for 2% of the time, Pallas kernels for 0%

profile of v4, /device:TPU:6, one launch (start us, length us, event | category | flops | bytes accessed | tf_op | source)
XLA Modules:
  0.0 166.0 jit_solution(12937655248027100463)
XLA Ops:
  6.5 0.7 fusion.45
  7.3 0.1 copy.58
  7.3 0.1 eq.84
  7.4 0.7 fusion.46
  8.1 0.1 copy.57
  8.2 0.1 squeeze.31
  8.3 0.7 pad_clamp_fusion.2
  9.0 0.8 slice_bitcast_fusion.1
  9.7 0.7 gather_fusion
  10.4 0.1 broadcast_in_dim.54
  10.5 0.1 and.64
  10.6 0.1 fusion.17
  10.7 0.2 reduce_window_sum.31
  10.9 0.2 select_reduce_fusion.1
  11.1 0.1 reduce_sum.41
  11.1 0.1 fusion.33
  11.2 0.1 fusion.13
  11.4 1.0 convolution_convert_fusion.1
  12.3 0.1 copy.44
  12.5 0.1 reshape.210
  12.6 0.1 copy.60
  12.7 0.1 eq.93
  12.7 0.1 copy.59
  12.8 0.1 squeeze.34
  12.9 0.7 gather_fusion.1
  13.6 0.1 broadcast_in_dim.57
  13.7 0.1 and.69
  13.8 0.1 fusion.19
  13.9 0.2 reduce_window_sum.32
  14.1 0.2 select_reduce_fusion
  14.2 0.1 reduce_sum.43
  14.3 0.1 fusion.37
  14.4 0.1 fusion.14
  14.5 0.3 convolution_convert_fusion
  14.8 0.1 copy.49
  15.0 0.1 reshape.211
  15.1 0.3 pad_maximum_fusion.1
  15.4 36.2 %all_to_all.15 = bf16[64,8,448]{2,1,0:T(8,128)(2,1)S(1)} all-to-all(bf16[64,8,448]{2,1,0:T(8,128)(2,1)S(1)} %pad_maximum_fusion.1), channel_id=1, replica_groups=mesh['expert'=64,'tensor'=8] {'expert'}, dimensions={0} | all-to-all | bytes 917504 | tf_op jit(solution)/shard_map/all_to_all | solution.py:71
  51.6 0.9 pad_maximum_fusion
  52.5 29.7 %all-gather.5.cloned.1.call-done = bf16[4352,448]{1,0:T(8,128)(2,1)} async-done(((bf16[544,448]{1,0:T(8,128)(2,1)}), bf16[4352,448]{1,0:T(8,128)(2,1)}) %all-gather.5.cloned.1.call-update) | async-done | bytes 3899408 | tf_op jit(solution)/shard_map/all_gather | solution.py:77
  82.2 3.6 %multiply_convert_fusion = bf16[544,256]{1,0:T(8,128)(2,1)S(1)} fusion(bf16[8,544,448]{2,1,0:T(8,128)(2,1)} %bitcast.50, bf16[8,448,128]{2,1,0:T(8,128)(2,1)S(1)} %bitcast.53, bf16[8,448,128]{2,1,0:T(8,128)(2,1)S(1)} %bitcast.54), kind=kOutput, calls=%fused_computation.19 | convolution fusion | flops 1002610688 | bytes 6012928 | tf_op jit(solution)/shard_map/tmc,tch->mh/dot_general | solution.py:79
  85.8 0.8 slice_select_fusion
  86.7 0.7 copy.50
  87.4 0.7 copy.51
  88.1 0.2 maximum_bitcast_fusion
  88.3 32.0 %all_to_all.16 = bf16[8,256,448]{1,2,0:T(8,128)(2,1)S(1)} all-to-all(bf16[8,256,448]{1,2,0:T(8,128)(2,1)S(1)} %maximum_bitcast_fusion), channel_id=1, replica_groups=mesh['expert'=64,'tensor'=8] {'tensor'}, dimensions={0} | all-to-all | bytes 3670016 | tf_op jit(solution)/shard_map/all_to_all | solution.py:63
  120.3 1.9 %fusion.4 = bf16[512,448]{0,1:T(8,128)(2,1)S(1)} fusion(bf16[8,544,128]{2,1,0:T(8,128)(2,1)} %bitcast.51, bf16[8,256,448]{1,2,0:T(8,128)(2,1)S(1)} %all_to_all.16), kind=kOutput, calls=%fused_computation.10 | convolution fusion | flops 469991424 | bytes 2424832 | tf_op jit(solution)/shard_map/imu,iuc->mc/dot_general | solution.py:84
  122.2 1.0 copy.52
  123.2 13.3 %all-to-all-start.2 = ((bf16[64,8,448]{2,1,0:T(8,128)(2,1)}), bf16[64,8,448]{2,1,0:T(8,128)(2,1)S(1)}, u32[]{:S(2)}, u32[]{:S(2)}) async-start(bf16[64,8,448]{2,1,0:T(8,128)(2,1)} %bitcast.17), calls=%async_computation.2 | async-start | bytes 1048576 | tf_op jit(solution)/shard_map/all_to_all | solution.py:96
  136.6 0.1 mul.101
  136.7 0.1 copy.54
  136.7 0.1 squeeze.37
  136.9 0.1 mul.93
  137.1 0.1 squeeze.36
  137.2 1.2 convolution_bitcast_fusion.1
  138.4 17.7 %all-to-all-done.2 = bf16[64,8,448]{2,1,0:T(8,128)(2,1)S(1)} async-done(((bf16[64,8,448]{2,1,0:T(8,128)(2,1)}), bf16[64,8,448]{2,1,0:T(8,128)(2,1)S(1)}, u32[]{:S(2)}, u32[]{:S(2)}) %all-to-all-start.2) | async-done | bytes 458784 | tf_op jit(solution)/shard_map/all_to_all | solution.py:96
  156.1 0.2 fusion.43
  156.3 0.1 reshape.215
  156.4 0.1 reshape.217
  156.5 0.8 gather_fusion.2
  157.4 0.8 gather_fusion.3
  158.2 0.2 bitcast_reduce_fusion
  158.5 0.1 fusion.24
  158.6 0.6 pad_maximum_fusion.2
  (34 shorter events, 0.4 us)
Async XLA Ops:
  6.5 8.0 %copy-start.2 = (bf16[2,16,448]{2,1,0:T(8,128)(2,1)S(1)}, bf16[2,16,448]{2,1,0:T(8,128)(2,1)}, u32[]{:S(2)}) copy-start(bf16[2,16,448]{2,1,0:T(8,128)(2,1)} %param.17) | copy-start | bytes 86020
  6.5 75.7 %all-gather.5.cloned.1.call-start = ((), (), s32[]{:S(2)}) async-start(), calls=%async_computation.3 | async-start | bytes 5013504 | tf_op jit(solution)/shard_map/all_gather | solution.py:77
  15.0 67.2 %copy-start.4 = (bf16[3584,128]{1,0:T(8,128)(2,1)S(1)}, bf16[3584,128]{1,0:T(8,128)(2,1)}, u32[]{:S(2)}) copy-start(bf16[3584,128]{1,0:T(8,128)(2,1)} %param.24) | copy-start | bytes 2752516
  15.1 67.2 %copy-start.5 = (bf16[1,3584,128]{2,1,0:T(8,128)(2,1)S(1)}, bf16[1,3584,128]{2,1,0:T(8,128)(2,1)}, u32[]{:S(2)}) copy-start(bf16[1,3584,128]{2,1,0:T(8,128)(2,1)} %param.22) | copy-start | bytes 2752516
  52.5 67.8 %all-gather.7.cloned.1.call-start = ((), (), s32[]{:S(2)}) async-start(), calls=%async_computation.4 | async-start | bytes 1253376 | tf_op jit(solution)/shard_map/all_gather | solution.py:83
  82.2 4.4 %copy-start = (bf16[1,128,3584]{2,1,0:T(8,128)(2,1)S(1)}, bf16[1,128,3584]{2,1,0:T(8,128)(2,1)}, u32[]{:S(2)}) copy-start(bf16[1,128,3584]{2,1,0:T(8,128)(2,1)} %param.23) | copy-start | bytes 2752516
  85.8 1.5 copy-start.1
  122.2 14.3 %copy-start.3 = (f32[2,16,8]{1,2,0:T(8,128)S(1)}, f32[2,16,8]{1,2,0:T(8,128)}, u32[]{:S(2)}) copy-start(f32[2,16,8]{1,2,0:T(8,128)} %param.21) | copy-start | bytes 3076
  123.2 32.9 %all-to-all-start.2 = ((bf16[64,8,448]{2,1,0:T(8,128)(2,1)}), bf16[64,8,448]{2,1,0:T(8,128)(2,1)S(1)}, u32[]{:S(2)}, u32[]{:S(2)}) async-start(bf16[64,8,448]{2,1,0:T(8,128)(2,1)} %bitcast.17), calls=%async_computation.2 | async-start | bytes 1048576 | tf_op jit(solution)/shard_map/all_to_all | solution.py:96
Sparse Core Ops, SparseCore 0:
  52.6 29.5 all-gather.4
  86.8 33.4 all-gather.6

commit v5 on v4

--- a/solution.py
+++ b/solution.py
@@ -60,7 +60,12 @@
     hidden_units = slot_up.shape[2]
     down_parts = jnp.concatenate([slot_down[0], shared_down], axis=0)
     down_parts = down_parts.reshape(-1, tensor_count, width_part).transpose(1, 0, 2)
-    down_cols = lax.all_to_all(down_parts, "tensor", split_axis=0, concat_axis=0, tiled=True)
+    me = lax.axis_index("tensor")
+    received_parts = [lax.dynamic_index_in_dim(down_parts, me, 0, keepdims=False)]
+    for shift in range(1, tensor_count):
+        piece = lax.dynamic_index_in_dim(down_parts, (me + shift) % tensor_count, 0, keepdims=False)
+        pairs = [(i, (i + shift) % tensor_count) for i in range(tensor_count)]
+        received_parts.append(lax.ppermute(piece, "tensor", pairs))
     outgoing = []
     for index in range(step_count):
         packed = jnp.dot(
@@ -81,18 +86,20 @@
     is_routed = (jnp.arange(served + own) < served)[:, None]
     act_own = jnp.where(is_routed, act[:, :hidden_units], act[:, hidden_units:])
     act_all = lax.all_gather(act_own, "tensor", axis=0, tiled=False)
-    routed_back = jnp.einsum(
-        "imu,iuc->mc",
-        act_all[:, :served],
-        down_cols[:, :hidden_units],
-        preferred_element_type=jnp.float32,
-    ).astype(jnp.bfloat16).reshape(received.shape)
-    shared_own = jnp.einsum(
-        "imu,iuc->mc",
-        act_all[:, served:],
-        down_cols[:, hidden_units:],
-        preferred_element_type=jnp.float32,
-    ).reshape(step_count, row_count, width_part)
+    routed_sum = None
+    shared_sum = None
+    for shift, part in enumerate(received_parts):
+        act_part = lax.dynamic_index_in_dim(act_all, (me - shift) % tensor_count, 0, keepdims=False)
+        routed_term = jnp.dot(
+            act_part[:served], part[:hidden_units], preferred_element_type=jnp.float32
+        )
+        shared_term = jnp.dot(
+            act_part[served:], part[hidden_units:], preferred_element_type=jnp.float32
+        )
+        routed_sum = routed_term if routed_sum is None else routed_sum + routed_term
+        shared_sum = shared_term if shared_sum is None else shared_sum + shared_term
+    routed_back = routed_sum.astype(jnp.bfloat16).reshape(received.shape)
+    shared_own = shared_sum.reshape(step_count, row_count, width_part)
     answer = lax.all_to_all(routed_back, "expert", split_axis=0, concat_axis=0, tiled=True)
     results = []
     for index in range(step_count):

time: 168 us -> 187 us (1.11)
  blocking collectives: 68.2 us -> 36.2 us
  waiting for transfers between devices: 47.4 us -> 76.7 us
  starting transfers between devices: 13.3 us -> 30 us
  matrix products: 7.93 us -> 12.7 us
    all_to_all x1 -> x0, blocking collectives: 32 us -> none  [layer(): lax.all_to_all(down_parts, 'tensor', split_axis=0, concat_axis=0, tiled=T...]
    ppermute x0 -> x7, starting transfers between devices: none -> 16.6 us  [layer(): received_parts.append(lax.ppermute(piece, 'tensor', pairs))]
    all_gather x1, waiting for transfers between devices: 0.01 us -> 16 us  [layer(): act_all = lax.all_gather(act_own, 'tensor', axis=0, tiled=False)]
    ppermute x0 -> x7, waiting for transfers between devices: none -> 15.6 us  [layer(): received_parts.append(lax.ppermute(piece, 'tensor', pairs))]
    dot_general x2 -> x16, matrix products: 3.1 us -> 8.32 us  [the longest x8 5.22 us: layer(): jnp.dot(act_part[:served], part[:hidden_units], preferred_element_type=jn...]
    all_to_all x1, waiting for transfers between devices: 17.7 us -> 15.4 us  [layer(): lax.all_to_all(routed_back, 'expert', split_axis=0, concat_axis=0, tiled=...]
  transfers between devices with their start and end apart: 3 -> 10, of which waited for: 2 -> 5; matrix products, arithmetic and copies ran while one was open for 2% -> 5% of each run, Pallas kernels for 0% -> 0%
where the time goes in v5:
time: 187 us; the launch traced here: 186 us
  waiting for transfers between devices  76.7 us (41%)
  blocking collectives  36.2 us (19%)
  starting transfers between devices  30 us (16%)
  between operations  14.2 us (8%)
  matrix products  12.7 us (7%)
  local copies, waits for them, and re-layouts  9.93 us (5%)
  other arithmetic  6.03 us (3%)
    all_to_all x1, blocking collectives, layer(): lax.all_to_all(batch, 'expert', split_axis=0, concat_axis=0, tiled=True)  36.2 us
    all_gather x1, waiting for transfers between devices, layer(): rows_all = lax.all_gather(rows_part, 'tensor', axis=0, tiled=False)  29.7 us
    ppermute x7, starting transfers between devices, layer(): received_parts.append(lax.ppermute(piece, 'tensor', pairs))  16.6 us
    all_gather x1, waiting for transfers between devices, layer(): act_all = lax.all_gather(act_own, 'tensor', axis=0, tiled=False)  16 us
    ppermute x7, waiting for transfers between devices, layer(): received_parts.append(lax.ppermute(piece, 'tensor', pairs))  15.6 us
    all_to_all x1, waiting for transfers between devices, layer(): lax.all_to_all(routed_back, 'expert', split_axis=0, concat_axis=0, tiled=...  15.4 us
    all_to_all x1, starting transfers between devices, layer(): lax.all_to_all(routed_back, 'expert', split_axis=0, concat_axis=0, tiled=...  13.4 us
    dot_general x8, matrix products, layer(): jnp.dot(act_part[:served], part[:hidden_units], preferred_element_type=jn...  5.22 us
  transfers between devices with their start and end apart: 10, of which 5 were waited for; matrix products, arithmetic and copies ran while one was open for 5% of the time, Pallas kernels for 0%

profile of v5, /device:TPU:6, one launch (start us, length us, event | category | flops | bytes accessed | tf_op | source)
XLA Modules:
  0.0 185.8 jit_solution(13553838048365609295)
XLA Ops:
  6.5 0.8 slice_bitcast_fusion.5
  7.3 0.7 pad_clamp_fusion.2
  8.0 0.7 gather_fusion.1
  8.6 0.7 gather_fusion
  9.4 0.1 and.131
  9.6 0.1 and.126
  9.7 0.7 fusion.110
  11.2 0.2 reduce_window_sum.32
  11.4 0.2 select_reduce_fusion
  11.7 0.1 fusion.43
  12.0 0.2 reduce_window_sum.31
  12.1 0.2 select_reduce_fusion.1
  12.5 0.1 fusion.42
  12.6 0.3 convolution_convert_fusion.1
  12.9 0.1 copy.42
  13.1 0.3 convolution_convert_fusion
  13.4 0.1 copy.47
  13.6 0.3 pad_maximum_fusion.1
  13.9 36.2 %all_to_all.10 = bf16[64,8,448]{2,1,0:T(8,128)(2,1)S(1)} all-to-all(bf16[64,8,448]{2,1,0:T(8,128)(2,1)S(1)} %pad_maximum_fusion.1), channel_id=1, replica_groups=mesh['expert'=64,'tensor'=8] {'expert'}, dimensions={0} | all-to-all | bytes 917504 | tf_op jit(solution)/shard_map/all_to_all | solution.py:76
  50.2 0.9 pad_maximum_fusion
  51.1 29.7 %all-gather.5.cloned.1.call-done = bf16[4352,448]{1,0:T(8,128)(2,1)} async-done(((bf16[544,448]{1,0:T(8,128)(2,1)}), bf16[4352,448]{1,0:T(8,128)(2,1)}) %all-gather.5.cloned.1.call-update) | async-done | bytes 3899408 | tf_op jit(solution)/shard_map/all_gather | solution.py:82
  80.8 3.8 %multiply_convert_fusion = bf16[544,256]{1,0:T(8,128)(2,1)S(1)} fusion(bf16[8,544,448]{2,1,0:T(8,128)(2,1)} %bitcast.130, bf16[8,448,128]{2,1,0:T(8,128)(2,1)S(1)} %bitcast.131, bf16[8,448,128]{2,1,0:T(8,128)(2,1)} %bitcast.132), kind=kOutput, calls=%fused_computation.43 | convolution fusion | flops 1002610688 | bytes 6012928 | tf_op jit(solution)/shard_map/tmc,tch->mh/dot_general | solution.py:84
  84.6 0.8 slice_select_fusion
  85.5 0.6 copy.48
  86.1 0.5 copy-done.2
  86.6 0.6 copy.49
  87.2 0.8 fusion.28
  88.1 3.3 %collective-permute-start.5 = (bf16[256,448]{0,1:T(8,128)(2,1)}, bf16[256,448]{0,1:T(8,128)(2,1)S(1)}, u32[]{:S(2)}, u32[]{:S(2)}) collective-permute-start(bf16[256,448]{0,1:T(8,128)(2,1)} %get-tuple-element.37), channel_id=1, source_target_pairs={{0,6},{1,7},{2,0},{3,1},{4,2},{5,3},{6,4},{7,5},{8,14},{9,15},{10,... | collective-permute-start | bytes 688136 | tf_op jit(solution)/shard_map/ppermute | solution.py:68
  91.4 0.4 collective-permute-start.6
  91.8 0.2 fusion.32
  92.0 4.3 %collective-permute-start.1 = (bf16[256,448]{0,1:T(8,128)(2,1)S(1)}, bf16[256,448]{0,1:T(8,128)(2,1)}, u32[]{:S(2)}, u32[]{:S(2)}) collective-permute-start(bf16[256,448]{0,1:T(8,128)(2,1)S(1)} %get-tuple-element.31), channel_id=1, source_target_pairs={{0,2},{1,3},{2,4},{3,5},{4,6},{5,7},{6,0},{7,1},{8,10},{9,11},{10,... | collective-permute-start | bytes 688136 | tf_op jit(solution)/shard_map/ppermute | solution.py:68
  96.3 3.4 %collective-permute-start.2 = (bf16[256,448]{0,1:T(8,128)(2,1)S(1)}, bf16[256,448]{0,1:T(8,128)(2,1)S(1)}, u32[]{:S(2)}, u32[]{:S(2)}) collective-permute-start(bf16[256,448]{0,1:T(8,128)(2,1)S(1)} %get-tuple-element.34), channel_id=1, source_target_pairs={{0,3},{1,4},{2,5},{3,6},{4,7},{5,0},{6,1},{7,2},{8,11},{9,12},{10,... | collective-permute-start | bytes 688136 | tf_op jit(solution)/shard_map/ppermute | solution.py:68
  100.6 16.0 %all-gather.7.cloned.1.call-done = bf16[4352,128]{1,0:T(8,128)(2,1)} async-done(((bf16[544,128]{1,0:T(8,128)(2,1)}), bf16[4352,128]{1,0:T(8,128)(2,1)}) %all-gather.7.cloned.1.call-update) | async-done | bytes 1114128 | tf_op jit(solution)/shard_map/all_gather | solution.py:88
  116.6 1.3 fusion.41
  117.9 3.2 %collective-permute-start.4 = (bf16[256,448]{0,1:T(8,128)(2,1)S(1)}, bf16[256,448]{0,1:T(8,128)(2,1)S(1)}, u32[]{:S(2)}, u32[]{:S(2)}) collective-permute-start(bf16[256,448]{0,1:T(8,128)(2,1)S(1)} %get-tuple-element.36), channel_id=1, source_target_pairs={{0,5},{1,6},{2,7},{3,0},{4,1},{5,2},{6,3},{7,4},{8,13},{9,14},{10,... | collective-permute-start | bytes 688136 | tf_op jit(solution)/shard_map/ppermute | solution.py:68
  121.1 0.3 convolution_add_fusion.1
  121.4 7.5 %collective-permute-done.4 = bf16[256,448]{0,1:T(8,128)(2,1)S(1)} collective-permute-done((bf16[256,448]{0,1:T(8,128)(2,1)S(1)}, bf16[256,448]{0,1:T(8,128)(2,1)S(1)}, u32[]{:S(2)}, u32[]{:S(2)}) %collective-permute-start.4) | collective-permute-done | bytes 229408 | tf_op jit(solution)/shard_map/ppermute | solution.py:68
  128.9 1.9 %collective-permute-start.3 = (bf16[256,448]{0,1:T(8,128)(2,1)S(1)}, bf16[256,448]{0,1:T(8,128)(2,1)S(1)}, u32[]{:S(2)}, u32[]{:S(2)}) collective-permute-start(bf16[256,448]{0,1:T(8,128)(2,1)S(1)} %get-tuple-element.35), channel_id=1, source_target_pairs={{0,4},{1,5},{2,6},{3,7},{4,0},{5,1},{6,2},{7,3},{8,12},{9,13},{10,... | collective-permute-start | bytes 688136 | tf_op jit(solution)/shard_map/ppermute | solution.py:68
  130.8 0.3 fusion.38
  131.1 8.1 %collective-permute-done.3 = bf16[256,448]{0,1:T(8,128)(2,1)S(1)} collective-permute-done((bf16[256,448]{0,1:T(8,128)(2,1)S(1)}, bf16[256,448]{0,1:T(8,128)(2,1)S(1)}, u32[]{:S(2)}, u32[]{:S(2)}) %collective-permute-start.3) | collective-permute-done | bytes 229408 | tf_op jit(solution)/shard_map/ppermute | solution.py:68
  139.3 0.3 fusion.39
  139.6 0.3 fusion.40
  139.9 1.2 fusion.36
  141.1 0.3 fusion.37
  141.4 0.2 fusion.56
  141.6 1.3 fusion.9
  142.9 1.0 copy.50
  143.9 13.4 %all-to-all-start.1 = ((bf16[64,8,448]{2,1,0:T(8,128)(2,1)}), bf16[64,8,448]{2,1,0:T(8,128)(2,1)S(1)}, u32[]{:S(2)}, u32[]{:S(2)}) async-start(bf16[64,8,448]{2,1,0:T(8,128)(2,1)} %bitcast.32), calls=%async_computation.1 | async-start | bytes 1048576 | tf_op jit(solution)/shard_map/all_to_all | solution.py:103
  157.3 0.2 fusion.46
  157.5 1.1 fusion.44
  158.6 0.2 fusion.52
  158.7 0.2 fusion.50
  158.9 0.2 fusion.48
  159.1 0.2 convolution_add_fusion.3
  159.3 1.1 fusion.17
  160.3 15.4 %all-to-all-done.1 = bf16[64,8,448]{2,1,0:T(8,128)(2,1)S(1)} async-done(((bf16[64,8,448]{2,1,0:T(8,128)(2,1)}), bf16[64,8,448]{2,1,0:T(8,128)(2,1)S(1)}, u32[]{:S(2)}, u32[]{:S(2)}) %all-to-all-start.1) | async-done | bytes 458784 | tf_op jit(solution)/shard_map/all_to_all | solution.py:103
  175.8 0.2 fusion.107
  175.9 0.1 reshape.248
  176.1 0.1 reshape.250
  176.2 0.8 gather_fusion.2
  177.1 0.8 gather_fusion.3
  177.9 0.2 bitcast_reduce_fusion.1
  178.1 0.2 bitcast_reduce_fusion
  178.3 0.6 pad_maximum_fusion.2
  (72 shorter events, 2.5 us)
Async XLA Ops:
  6.5 4.2 %copy-start.8 = (s32[2,16,8]{1,2,0:T(8,128)S(1)}, s32[2,16,8]{1,2,0:T(8,128)}, u32[]{:S(2)}) copy-start(s32[2,16,8]{1,2,0:T(8,128)} %param.20) | copy-start | bytes 3076
  6.5 6.1 %copy-start.7 = (bf16[2,16,448]{2,1,0:T(8,128)(2,1)S(1)}, bf16[2,16,448]{2,1,0:T(8,128)(2,1)}, u32[]{:S(2)}) copy-start(bf16[2,16,448]{2,1,0:T(8,128)(2,1)} %param.17) | copy-start | bytes 86020
  6.5 74.3 %all-gather.5.cloned.1.call-start = ((), (), s32[]{:S(2)}) async-start(), calls=%async_computation.2 | async-start | bytes 5013504 | tf_op jit(solution)/shard_map/all_gather | solution.py:82
  13.9 66.9 %copy-start.10 = (bf16[3584,128]{1,0:T(8,128)(2,1)S(1)}, bf16[3584,128]{1,0:T(8,128)(2,1)}, u32[]{:S(2)}) copy-start(bf16[3584,128]{1,0:T(8,128)(2,1)} %param.24) | copy-start | bytes 2752516
  51.1 65.5 %all-gather.7.cloned.1.call-start = ((), (), s32[]{:S(2)}) async-start(), calls=%async_computation.3 | async-start | bytes 1253376 | tf_op jit(solution)/shard_map/all_gather | solution.py:88
  80.8 4.7 %copy-start.1 = (bf16[1,128,3584]{2,1,0:T(8,128)(2,1)S(1)}, bf16[1,128,3584]{2,1,0:T(8,128)(2,1)}, u32[]{:S(2)}) copy-start(bf16[1,128,3584]{2,1,0:T(8,128)(2,1)} %param.23) | copy-start | bytes 2752516
  85.4 1.2 copy-start.2
  88.1 53.0 %collective-permute-start.5 = (bf16[256,448]{0,1:T(8,128)(2,1)}, bf16[256,448]{0,1:T(8,128)(2,1)S(1)}, u32[]{:S(2)}, u32[]{:S(2)}) collective-permute-start(bf16[256,448]{0,1:T(8,128)(2,1)} %get-tuple-element.37), channel_id=1, source_target_pairs={{0,6},{1,7},{2,0},{3,1},{4,2},{5,3},{6,4},{7,5},{8,14},{9,15},{10,... | collective-permute-start | bytes 688136 | tf_op jit(solution)/shard_map/ppermute | solution.py:68
  91.4 48.5 %collective-permute-start.6 = (bf16[256,448]{0,1:T(8,128)(2,1)}, bf16[256,448]{0,1:T(8,128)(2,1)}, u32[]{:S(2)}, u32[]{:S(2)}) collective-permute-start(bf16[256,448]{0,1:T(8,128)(2,1)} %get-tuple-element.38), channel_id=1, source_target_pairs={{0,7},{1,0},{2,1},{3,2},{4,3},{5,4},{6,5},{7,6},{8,15},{9,8},{10,9... | collective-permute-start | bytes 688136 | tf_op jit(solution)/shard_map/ppermute | solution.py:68
  91.8 8.4 %copy-start.9 = (f32[2,16,8]{1,2,0:T(8,128)S(1)}, f32[2,16,8]{1,2,0:T(8,128)}, u32[]{:S(2)}) copy-start(f32[2,16,8]{1,2,0:T(8,128)} %param.21) | copy-start | bytes 3076
  92.0 49.6 %collective-permute-start.1 = (bf16[256,448]{0,1:T(8,128)(2,1)S(1)}, bf16[256,448]{0,1:T(8,128)(2,1)}, u32[]{:S(2)}, u32[]{:S(2)}) collective-permute-start(bf16[256,448]{0,1:T(8,128)(2,1)S(1)} %get-tuple-element.31), channel_id=1, source_target_pairs={{0,2},{1,3},{2,4},{3,5},{4,6},{5,7},{6,0},{7,1},{8,10},{9,11},{10,... | collective-permute-start | bytes 688136 | tf_op jit(solution)/shard_map/ppermute | solution.py:68
  96.3 21.6 %collective-permute-start = (bf16[256,448]{0,1:T(8,128)(2,1)S(1)}, bf16[256,448]{0,1:T(8,128)(2,1)S(1)}, u32[]{:S(2)}, u32[]{:S(2)}) collective-permute-start(bf16[256,448]{0,1:T(8,128)(2,1)S(1)} %get-tuple-element.33), channel_id=1, source_target_pairs={{0,1},{1,2},{2,3},{3,4},{4,5},{5,6},{6,7},{7,0},{8,9},{9,10},{10,1... | collective-permute-start | bytes 688136 | tf_op jit(solution)/shard_map/ppermute | solution.py:68
  96.3 43.3 %collective-permute-start.2 = (bf16[256,448]{0,1:T(8,128)(2,1)S(1)}, bf16[256,448]{0,1:T(8,128)(2,1)S(1)}, u32[]{:S(2)}, u32[]{:S(2)}) collective-permute-start(bf16[256,448]{0,1:T(8,128)(2,1)S(1)} %get-tuple-element.34), channel_id=1, source_target_pairs={{0,3},{1,4},{2,5},{3,6},{4,7},{5,0},{6,1},{7,2},{8,11},{9,12},{10,... | collective-permute-start | bytes 688136 | tf_op jit(solution)/shard_map/ppermute | solution.py:68
  116.6 4.5 %copy-start = (bf16[4352,128]{1,0:T(8,128)(2,1)S(1)}, bf16[4352,128]{1,0:T(8,128)(2,1)}, u32[]{:S(2)}) copy-start(bf16[4352,128]{1,0:T(8,128)(2,1)} %all-gather.7.cloned.1.call-done) | copy-start | bytes 3342340
  117.9 13.2 %copy-start.5 = (bf16[256,448]{0,1:T(8,128)(2,1)}, bf16[256,448]{0,1:T(8,128)(2,1)S(1)}, u32[]{:S(2)}) copy-start(bf16[256,448]{0,1:T(8,128)(2,1)S(1)} %collective-permute-done) | copy-start | bytes 688132
  117.9 11.0 %collective-permute-start.4 = (bf16[256,448]{0,1:T(8,128)(2,1)S(1)}, bf16[256,448]{0,1:T(8,128)(2,1)S(1)}, u32[]{:S(2)}, u32[]{:S(2)}) collective-permute-start(bf16[256,448]{0,1:T(8,128)(2,1)S(1)} %get-tuple-element.36), channel_id=1, source_target_pairs={{0,5},{1,6},{2,7},{3,0},{4,1},{5,2},{6,3},{7,4},{8,13},{9,14},{10,... | collective-permute-start | bytes 688136 | tf_op jit(solution)/shard_map/ppermute | solution.py:68
  128.9 10.3 %collective-permute-start.3 = (bf16[256,448]{0,1:T(8,128)(2,1)S(1)}, bf16[256,448]{0,1:T(8,128)(2,1)S(1)}, u32[]{:S(2)}, u32[]{:S(2)}) collective-permute-start(bf16[256,448]{0,1:T(8,128)(2,1)S(1)} %get-tuple-element.35), channel_id=1, source_target_pairs={{0,4},{1,5},{2,6},{3,7},{4,0},{5,1},{6,2},{7,3},{8,12},{9,13},{10,... | collective-permute-start | bytes 688136 | tf_op jit(solution)/shard_map/ppermute | solution.py:68
  139.6 1.5 copy-start.3
  142.9 15.7 %copy-start.4 = (bf16[256,448]{0,1:T(8,128)(2,1)S(1)}, bf16[256,448]{0,1:T(8,128)(2,1)}, u32[]{:S(2)}) copy-start(bf16[256,448]{0,1:T(8,128)(2,1)} %copy-done.3) | copy-start | bytes 688132
  143.9 15.2 %copy-start.6 = (bf16[256,448]{0,1:T(8,128)(2,1)S(1)}, bf16[256,448]{0,1:T(8,128)(2,1)}, u32[]{:S(2)}) copy-start(bf16[256,448]{0,1:T(8,128)(2,1)} %copy-done.5) | copy-start | bytes 688132
  143.9 31.9 %all-to-all-start.1 = ((bf16[64,8,448]{2,1,0:T(8,128)(2,1)}), bf16[64,8,448]{2,1,0:T(8,128)(2,1)S(1)}, u32[]{:S(2)}, u32[]{:S(2)}) async-start(bf16[64,8,448]{2,1,0:T(8,128)(2,1)} %bitcast.32), calls=%async_computation.1 | async-start | bytes 1048576 | tf_op jit(solution)/shard_map/all_to_all | solution.py:103
Sparse Core Ops, SparseCore 0:
  51.2 29.5 all-gather.4
  85.6 30.9 all-gather.6

commit v6 on v3

v6 whole, which is shorter than its diff:
```python
import jax
import jax.numpy as jnp
from jax import lax
from jax.sharding import PartitionSpec as P


def route_plan(lengths, chosen, second, gains, slot_count, capacity):
    step_count, row_count, top_count = chosen.shape
    span_rows = row_count // lengths.shape[1]
    positions = jnp.arange(row_count, dtype=jnp.int32)
    limit = jnp.repeat(lengths, span_rows, axis=1, total_repeat_length=row_count)
    live_mask = positions[None, :] % span_rows < limit
    replicas = slot_count // 8
    experts_all = slot_count - replicas
    slot_index = jnp.where(
        (chosen < replicas) & (second == 1), chosen + experts_all, chosen
    ).reshape(step_count, -1)
    valid = jnp.broadcast_to(live_mask[:, :, None], chosen.shape).reshape(step_count, -1)
    onehot = (
        (slot_index[:, :, None] == jnp.arange(slot_count, dtype=jnp.int32)[None, None, :])
        & valid[:, :, None]
    ).astype(jnp.int32)
    earlier = jnp.cumsum(onehot, axis=1) - onehot
    order_rank = jnp.sum(earlier * onehot, axis=2)
    step_ids = jnp.arange(step_count, dtype=jnp.int32)[:, None]
    place = (slot_index * step_count + step_ids) * capacity + order_rank
    target = jnp.where(valid, place, -1).reshape(step_count, row_count, top_count)
    buffer_ids = jnp.arange(slot_count * step_count * capacity, dtype=jnp.int32)
    picker = jnp.any(
        target.reshape(step_count * row_count, top_count)[None, :, :]
        == buffer_ids[:, None, None],
        axis=2,
    ).astype(jnp.bfloat16)
    weights = gains * live_mask[:, :, None].astype(jnp.float32)
    return (live_mask, target, picker, weights)


def shards(
    hidden_rows,
    draft_len,
    expert_ids,
    replica,
    route_gain,
    slot_up,
    slot_down,
    shared_up,
    shared_down,
):
    slot_count = lax.axis_size("expert")
    tensor_count = lax.axis_size("tensor")
    step_count, row_count, width_part = hidden_rows.shape
    top_count = expert_ids.shape[2]
    capacity = row_count * top_count // (slot_count - slot_count // 8) + 2
    live_mask, target, picker, weights = route_plan(
        draft_len, expert_ids, replica, route_gain, slot_count, capacity
    )
    hidden_units = slot_up.shape[2]
    down_parts = jnp.concatenate([slot_down[0], shared_down], axis=0)
    down_parts = down_parts.reshape(-1, tensor_count, width_part).transpose(1, 0, 2)
    down_cols = lax.all_to_all(down_parts, "tensor", split_axis=0, concat_axis=0, tiled=True)
    batch = jnp.dot(
        picker,
        hidden_rows.reshape(step_count * row_count, width_part),
        preferred_element_type=jnp.float32,
    ).astype(jnp.bfloat16).reshape(slot_count, step_count * capacity, width_part)
    received = lax.all_to_all(batch, "expert", split_axis=0, concat_axis=0, tiled=True)
    served = received.shape[0] * received.shape[1]
    own = step_count * row_count
    rows_part = jnp.concatenate(
        [received.reshape(served, width_part), hidden_rows.reshape(own, width_part)], axis=0
    )
    rows_all = lax.all_gather(rows_part, "tensor", axis=0, tiled=False)
    up_w = jnp.concatenate([slot_up[0], shared_up], axis=1).reshape(tensor_count, width_part, -1)
    up_value = jnp.einsum("tmc,tch->mh", rows_all, up_w, preferred_element_type=jnp.float32)
    act = jax.nn.silu(up_value).astype(jnp.bfloat16)
    is_routed = (jnp.arange(served + own) < served)[:, None]
    act_own = jnp.where(is_routed, act[:, :hidden_units], act[:, hidden_units:])
    act_all = lax.all_gather(act_own, "tensor", axis=0, tiled=False)
    routed_back = jnp.einsum(
        "imu,iuc->mc",
        act_all[:, :served],
        down_cols[:, :hidden_units],
        preferred_element_type=jnp.float32,
    ).astype(jnp.bfloat16).reshape(received.shape)
    shared_own = jnp.einsum(
        "imu,iuc->mc",
        act_all[:, served:],
        down_cols[:, hidden_units:],
        preferred_element_type=jnp.float32,
    ).reshape(step_count, row_count, width_part)
    answer = lax.all_to_all(routed_back, "expert", split_axis=0, concat_axis=0, tiled=True)
    slot_rows = answer.reshape(-1, width_part)
    fetched = jnp.take(slot_rows, jnp.maximum(target, 0).reshape(-1), axis=0).astype(jnp.float32)
    fetched = fetched.reshape(step_count, row_count, top_count, width_part)
    routed = jnp.sum(fetched * weights[:, :, :, None], axis=2)
    live = live_mask.astype(jnp.float32)[:, :, None]
    return ((routed + shared_own) * live).astype(jnp.bfloat16)


def solution(mesh):
    return jax.shard_map(
        shards,
        mesh=mesh,
        in_specs=(
            P(None, "expert", "tensor"),
            P(None, "expert"),
            P(None, "expert", None),
            P(None, "expert", None),
            P(None, "expert", None),
            P("expert", None, "tensor"),
            P("expert", "tensor", None),
            P(None, "tensor"),
            P("tensor", None),
        ),
        out_specs=P(None, "expert", "tensor"),
        check_vma=False,
    )
```

time: 168 us -> 167 us (level)
  blocking collectives: 68.2 us -> 36.2 us
  waiting for transfers between devices: 47.4 us -> 76 us
  starting transfers between devices: 13.3 us -> 19.2 us
  local copies, waits for them, and re-layouts: 10.3 us -> 7.61 us
    all_to_all x1 -> x0, blocking collectives: 32 us -> none  [shards(): lax.all_to_all(down_parts, 'tensor', split_axis=0, concat_axis=0, tiled=T...]
    all_to_all x0 -> x1, waiting for transfers between devices: none -> 26.7 us  [shards(): lax.all_to_all(down_parts, 'tensor', split_axis=0, concat_axis=0, tiled=T...]
    all_to_all x0 -> x1, starting transfers between devices: none -> 5.91 us  [shards(): lax.all_to_all(down_parts, 'tensor', split_axis=0, concat_axis=0, tiled=T...]
    unnamed x18 -> x17, local copies, waits for them, and re-layouts: 1.68 us -> 3.57 us
    slice x6 -> x0, local copies, waits for them, and re-layouts: 1.75 us -> none  [the longest x1 0.71 us: shards(): replica[index]]
  transfers between devices with their start and end apart: 3 -> 4, of which waited for: 2 -> 4; matrix products, arithmetic and copies ran while one was open for 2% -> 3% of each run, Pallas kernels for 0% -> 0%
where the time goes in v6:
time: 167 us; the launch traced here: 166 us
  waiting for transfers between devices  76 us (46%)
  blocking collectives  36.2 us (22%)
  starting transfers between devices  19.2 us (11%)
  between operations  13.6 us (8%)
  matrix products  7.74 us (5%)
  local copies, waits for them, and re-layouts  7.61 us (5%)
  other arithmetic  5.66 us (3%)
    all_to_all x1, blocking collectives, shards(): lax.all_to_all(batch, 'expert', split_axis=0, concat_axis=0, tiled=True)  36.2 us
    all_gather x1, waiting for transfers between devices, shards(): rows_all = lax.all_gather(rows_part, 'tensor', axis=0, tiled=False)  29.7 us
    all_to_all x1, waiting for transfers between devices, shards(): lax.all_to_all(down_parts, 'tensor', split_axis=0, concat_axis=0, tiled=T...  26.7 us
    all_to_all x1, waiting for transfers between devices, shards(): lax.all_to_all(routed_back, 'expert', split_axis=0, concat_axis=0, tiled=...  18.1 us
    all_to_all x1, starting transfers between devices, shards(): lax.all_to_all(routed_back, 'expert', split_axis=0, concat_axis=0, tiled=...  13.3 us
    all_to_all x1, starting transfers between devices, shards(): lax.all_to_all(down_parts, 'tensor', split_axis=0, concat_axis=0, tiled=T...  5.91 us
    unnamed x17, local copies, waits for them, and re-layouts  3.57 us
    dot_general x1, matrix products, shards(): jnp.einsum('tmc,tch->mh', rows_all, up_w, preferred_element_type=jnp.floa...  3.56 us
  transfers between devices with their start and end apart: 4, of which 4 were waited for; matrix products, arithmetic and copies ran while one was open for 3% of the time, Pallas kernels for 0%

profile of v6, /device:TPU:6, one launch (start us, length us, event | category | flops | bytes accessed | tf_op | source)
XLA Modules:
  0.0 166.1 jit_solution(7501884693797982086)
XLA Ops:
  6.5 0.0 copy-start.2
  6.5 0.0 all-gather.5.cloned.1.call-start
  6.5 0.7 pad_clamp_fusion.1
  7.2 0.8 copy.55
  8.0 0.6 gather_fusion
  8.5 0.1 copy.56
  8.6 0.1 broadcast_in_dim.47
  8.7 0.1 and.44
  8.8 0.8 copy.57
  9.6 0.8 copy.58
  10.4 0.1 eq.38
  10.4 0.1 fusion.16
  10.6 0.2 reduce_window_sum.22
  10.8 0.2 select_reduce_fusion
  11.0 0.1 reduce_sum.24
  11.1 0.1 copy.62
  11.2 0.1 gather.13
  11.2 0.1 lt.80
  11.3 0.1 copy.69
  11.4 0.1 add.96
  11.5 0.1 copy.63
  11.6 0.2 fusion.14
  11.8 1.1 convolution_convert_fusion
  12.9 0.0 copy-start.4
  12.9 0.2 copy.64
  13.1 0.0 copy-start.5
  13.2 36.2 %all_to_all.15 = bf16[64,8,448]{2,1,0:T(8,128)(2,1)S(1)} all-to-all(bf16[64,8,448]{2,1,0:T(8,128)(2,1)S(1)} %bitcast.39), channel_id=1, replica_groups=mesh['expert'=64,'tensor'=8] {'expert'}, dimensions={0} | all-to-all | bytes 917504 | tf_op jit(solution)/shard_map/all_to_all | solution.py:66
  49.4 0.0 copy-done.2
  49.4 0.9 pad_maximum_fusion
  50.3 0.0 all-gather.5.cloned.1.call-update
  50.3 0.0 all-gather.7.cloned.1.call-start
  50.3 29.7 %all-gather.5.cloned.1.call-done = bf16[4352,448]{1,0:T(8,128)(2,1)} async-done(((bf16[544,448]{1,0:T(8,128)(2,1)}), bf16[4352,448]{1,0:T(8,128)(2,1)}) %all-gather.5.cloned.1.call-update) | async-done | bytes 3899408 | tf_op jit(solution)/shard_map/all_gather | solution.py:72
  80.0 0.0 copy-done.4
  80.0 0.0 copy-done.5
  80.1 0.0 copy-start
  80.1 3.6 %multiply_convert_fusion = bf16[544,256]{1,0:T(8,128)(2,1)S(1)} fusion(bf16[8,544,448]{2,1,0:T(8,128)(2,1)} %bitcast.47, bf16[8,448,128]{2,1,0:T(8,128)(2,1)S(1)} %bitcast.50, bf16[8,448,128]{2,1,0:T(8,128)(2,1)S(1)} %bitcast.51), kind=kOutput, calls=%fused_computation.16 | convolution fusion | flops 1002610688 | bytes 6012928 | tf_op jit(solution)/shard_map/tmc,tch->mh/dot_general | solution.py:74
  83.6 0.0 copy-start.1
  83.6 0.8 slice_select_fusion
  84.4 0.0 all-gather.7.cloned.1.call-update
  84.5 0.0 copy-done
  84.5 0.6 copy.65
  85.1 0.0 copy-done.1
  85.1 0.6 copy.66
  85.7 1.4 maximum_bitcast_fusion
  87.2 5.9 %all-to-all-start.1 = ((bf16[8,256,448]{1,2,0:T(8,128)(2,1)}), bf16[8,256,448]{1,2,0:T(8,128)(2,1)S(1)}, u32[]{:S(2)}, u32[]{:S(2)}) async-start(bf16[8,256,448]{1,2,0:T(8,128)(2,1)} %maximum_bitcast_fusion), calls=%async_computation.1 | async-start | bytes 3670016 | tf_op jit(solution)/shard_map/all_to_all | solution.py:60
  93.1 0.1 reduce_sum.23
  93.2 26.7 %all-to-all-done.1 = bf16[8,256,448]{1,2,0:T(8,128)(2,1)S(1)} async-done(((bf16[8,256,448]{1,2,0:T(8,128)(2,1)}), bf16[8,256,448]{1,2,0:T(8,128)(2,1)S(1)}, u32[]{:S(2)}, u32[]{:S(2)}) %all-to-all-start.1) | async-done | bytes 1835040 | tf_op jit(solution)/shard_map/all_to_all | solution.py:60
  119.8 1.5 all-gather.7.cloned.1.call-done
  121.4 1.9 %fusion.4 = bf16[512,448]{0,1:T(8,128)(2,1)S(1)} fusion(bf16[8,544,128]{2,1,0:T(8,128)(2,1)} %bitcast.48, bf16[8,256,448]{1,2,0:T(8,128)(2,1)S(1)} %all-to-all-done.1), kind=kOutput, calls=%fused_computation.8 | convolution fusion | flops 469991424 | bytes 2424832 | tf_op jit(solution)/shard_map/imu,iuc->mc/dot_general | solution.py:79
  123.3 0.0 copy-start.3
  123.3 1.0 copy.67
  124.3 13.3 %all-to-all-start.2 = ((bf16[64,8,448]{2,1,0:T(8,128)(2,1)}), bf16[64,8,448]{2,1,0:T(8,128)(2,1)S(1)}, u32[]{:S(2)}, u32[]{:S(2)}) async-start(bf16[64,8,448]{2,1,0:T(8,128)(2,1)} %bitcast.14), calls=%async_computation.2 | async-start | bytes 1048576 | tf_op jit(solution)/shard_map/all_to_all | solution.py:91
  137.6 0.1 broadcast_compare_fusion
  137.7 0.1 reshape.226
  137.8 0.0 copy-done.3
  137.8 0.1 copy.68
  137.9 1.2 fusion.9
  139.1 18.1 %all-to-all-done.2 = bf16[64,8,448]{2,1,0:T(8,128)(2,1)S(1)} async-done(((bf16[64,8,448]{2,1,0:T(8,128)(2,1)}), bf16[64,8,448]{2,1,0:T(8,128)(2,1)S(1)}, u32[]{:S(2)}, u32[]{:S(2)}) %all-to-all-start.2) | async-done | bytes 458784 | tf_op jit(solution)/shard_map/all_to_all | solution.py:91
  157.2 1.2 gather_fusion.1
  158.3 0.3 multiply_reduce_fusion
  158.6 0.7 multiply_convert_fusion.1
  (11 shorter events, 0.1 us)
Async XLA Ops:
  6.5 42.9 %copy-start.2 = (bf16[2,16,448]{2,1,0:T(8,128)(2,1)S(1)}, bf16[2,16,448]{2,1,0:T(8,128)(2,1)}, u32[]{:S(2)}) copy-start(bf16[2,16,448]{2,1,0:T(8,128)(2,1)} %param.11) | copy-start | bytes 86020
  6.5 73.5 %all-gather.5.cloned.1.call-start = ((), (), s32[]{:S(2)}) async-start(), calls=%async_computation.3 | async-start | bytes 5013504 | tf_op jit(solution)/shard_map/all_gather | solution.py:72
  12.9 67.1 %copy-start.4 = (bf16[3584,128]{1,0:T(8,128)(2,1)S(1)}, bf16[3584,128]{1,0:T(8,128)(2,1)}, u32[]{:S(2)}) copy-start(bf16[3584,128]{1,0:T(8,128)(2,1)} %param.18) | copy-start | bytes 2752516
  13.1 66.9 %copy-start.5 = (bf16[1,3584,128]{2,1,0:T(8,128)(2,1)S(1)}, bf16[1,3584,128]{2,1,0:T(8,128)(2,1)}, u32[]{:S(2)}) copy-start(bf16[1,3584,128]{2,1,0:T(8,128)(2,1)} %param.16) | copy-start | bytes 2752516
  50.3 71.1 %all-gather.7.cloned.1.call-start = ((), (), s32[]{:S(2)}) async-start(), calls=%async_computation.4 | async-start | bytes 1253376 | tf_op jit(solution)/shard_map/all_gather | solution.py:78
  80.1 4.4 %copy-start = (bf16[1,128,3584]{2,1,0:T(8,128)(2,1)S(1)}, bf16[1,128,3584]{2,1,0:T(8,128)(2,1)}, u32[]{:S(2)}) copy-start(bf16[1,128,3584]{2,1,0:T(8,128)(2,1)} %param.17) | copy-start | bytes 2752516
  83.6 1.5 copy-start.1
  87.2 32.7 %all-to-all-start.1 = ((bf16[8,256,448]{1,2,0:T(8,128)(2,1)}), bf16[8,256,448]{1,2,0:T(8,128)(2,1)S(1)}, u32[]{:S(2)}, u32[]{:S(2)}) async-start(bf16[8,256,448]{1,2,0:T(8,128)(2,1)} %maximum_bitcast_fusion), calls=%async_computation.1 | async-start | bytes 3670016 | tf_op jit(solution)/shard_map/all_to_all | solution.py:60
  123.3 14.5 %copy-start.3 = (f32[2,16,8]{1,2,0:T(8,128)S(1)}, f32[2,16,8]{1,2,0:T(8,128)}, u32[]{:S(2)}) copy-start(f32[2,16,8]{1,2,0:T(8,128)} %param.15) | copy-start | bytes 3076
  124.3 32.9 %all-to-all-start.2 = ((bf16[64,8,448]{2,1,0:T(8,128)(2,1)}), bf16[64,8,448]{2,1,0:T(8,128)(2,1)S(1)}, u32[]{:S(2)}, u32[]{:S(2)}) async-start(bf16[64,8,448]{2,1,0:T(8,128)(2,1)} %bitcast.14), calls=%async_computation.2 | async-start | bytes 1048576 | tf_op jit(solution)/shard_map/all_to_all | solution.py:91
Sparse Core Ops, SparseCore 0:
  50.4 29.5 all-gather.4
  84.6 36.7 all-gather.6

commit v7 on v6

--- a/solution.py
+++ b/solution.py
@@ -1,7 +1,9 @@
 import jax
 import jax.numpy as jnp
 from jax import lax
-from jax.sharding import PartitionSpec as P
+from jax.sharding import Mesh, PartitionSpec as P
+
+TENSOR = ("tx", "tc")
 
 
 def route_plan(lengths, chosen, second, gains, slot_count, capacity):
@@ -47,7 +49,9 @@
     shared_down,
 ):
     slot_count = lax.axis_size("expert")
-    tensor_count = lax.axis_size("tensor")
+    chips_x = lax.axis_size("tx")
+    cores = lax.axis_size("tc")
+    tensor_count = chips_x * cores
     step_count, row_count, width_part = hidden_rows.shape
     top_count = expert_ids.shape[2]
     capacity = row_count * top_count // (slot_count - slot_count // 8) + 2
@@ -57,7 +61,7 @@
     hidden_units = slot_up.shape[2]
     down_parts = jnp.concatenate([slot_down[0], shared_down], axis=0)
     down_parts = down_parts.reshape(-1, tensor_count, width_part).transpose(1, 0, 2)
-    down_cols = lax.all_to_all(down_parts, "tensor", split_axis=0, concat_axis=0, tiled=True)
+    down_cols = lax.all_to_all(down_parts, TENSOR, split_axis=0, concat_axis=0, tiled=True)
     batch = jnp.dot(
         picker,
         hidden_rows.reshape(step_count * row_count, width_part),
@@ -69,13 +73,19 @@
     rows_part = jnp.concatenate(
         [received.reshape(served, width_part), hidden_rows.reshape(own, width_part)], axis=0
     )
-    rows_all = lax.all_gather(rows_part, "tensor", axis=0, tiled=False)
-    up_w = jnp.concatenate([slot_up[0], shared_up], axis=1).reshape(tensor_count, width_part, -1)
-    up_value = jnp.einsum("tmc,tch->mh", rows_all, up_w, preferred_element_type=jnp.float32)
+    rows_x = lax.all_gather(rows_part, "tx", axis=0, tiled=False)
+    rows_sibling = lax.ppermute(rows_x, "tc", [(0, 1), (1, 0)])
+    core = lax.axis_index("tc")
+    up_w = jnp.concatenate([slot_up[0], shared_up], axis=1).reshape(chips_x, cores, width_part, -1)
+    up_own = lax.dynamic_index_in_dim(up_w, core, 1, keepdims=False)
+    up_sibling = lax.dynamic_index_in_dim(up_w, 1 - core, 1, keepdims=False)
+    up_value = jnp.einsum(
+        "xmc,xch->mh", rows_x, up_own, preferred_element_type=jnp.float32
+    ) + jnp.einsum("xmc,xch->mh", rows_sibling, up_sibling, preferred_element_type=jnp.float32)
     act = jax.nn.silu(up_value).astype(jnp.bfloat16)
     is_routed = (jnp.arange(served + own) < served)[:, None]
     act_own = jnp.where(is_routed, act[:, :hidden_units], act[:, hidden_units:])
-    act_all = lax.all_gather(act_own, "tensor", axis=0, tiled=False)
+    act_all = lax.all_gather(act_own, TENSOR, axis=0, tiled=False)
     routed_back = jnp.einsum(
         "imu,iuc->mc",
         act_all[:, :served],
@@ -98,20 +108,22 @@
 
 
 def solution(mesh):
+    expert_count, tensor_count = mesh.devices.shape
+    chip_mesh = Mesh(mesh.devices.reshape(expert_count, tensor_count // 2, 2), ("expert",) + TENSOR)
     return jax.shard_map(
         shards,
-        mesh=mesh,
+        mesh=chip_mesh,
         in_specs=(
-            P(None, "expert", "tensor"),
+            P(None, "expert", TENSOR),
             P(None, "expert"),
             P(None, "expert", None),
             P(None, "expert", None),
             P(None, "expert", None),
-            P("expert", None, "tensor"),
-            P("expert", "tensor", None),
-            P(None, "tensor"),
-            P("tensor", None),
+            P("expert", None, TENSOR),
+            P("expert", TENSOR, None),
+            P(None, TENSOR),
+            P(TENSOR, None),
         ),
-        out_specs=P(None, "expert", "tensor"),
+        out_specs=P(None, "expert", TENSOR),
         check_vma=False,
     )

time: 167 us -> 170 us (1.018)
    ppermute x0 -> x1, waiting for transfers between devices: none -> 2.24 us  [shards(): rows_sibling = lax.ppermute(rows_x, 'tc', [(0, 1), (1, 0)])]
    ppermute x0 -> x1, starting transfers between devices: none -> 1.91 us  [shards(): rows_sibling = lax.ppermute(rows_x, 'tc', [(0, 1), (1, 0)])]
    dot_general x1 -> x2, matrix products: 3.56 us -> 4.73 us  [the longest x1 2.37 us: shards(): jnp.einsum('xmc,xch->mh', rows_sibling, up_sibling, preferred_element_typ...]
  transfers between devices with their start and end apart: 4 -> 5, of which waited for: 4 -> 5; matrix products, arithmetic and copies ran while one was open for 3% -> 4% of each run, Pallas kernels for 0% -> 0%
where the time goes in v7:
time: 170 us; the launch traced here: 168 us
  waiting for transfers between devices  76.8 us (45%)
  blocking collectives  36.2 us (21%)
  starting transfers between devices  19.6 us (12%)
  between operations  13.6 us (8%)
  matrix products  8.91 us (5%)
  local copies, waits for them, and re-layouts  7.63 us (4%)
  other arithmetic  5.66 us (3%)
    all_to_all x1, blocking collectives, shards(): lax.all_to_all(batch, 'expert', split_axis=0, concat_axis=0, tiled=True)  36.2 us
    all_gather x1, waiting for transfers between devices, shards(): rows_x = lax.all_gather(rows_part, 'tx', axis=0, tiled=False)  28.4 us
    all_to_all x1, waiting for transfers between devices, shards(): lax.all_to_all(down_parts, TENSOR, split_axis=0, concat_axis=0, tiled=True)  26.7 us
    all_to_all x1, waiting for transfers between devices, shards(): lax.all_to_all(routed_back, 'expert', split_axis=0, concat_axis=0, tiled=...  17.9 us
    all_to_all x1, starting transfers between devices, shards(): lax.all_to_all(routed_back, 'expert', split_axis=0, concat_axis=0, tiled=...  11.7 us
    all_to_all x1, starting transfers between devices, shards(): lax.all_to_all(down_parts, TENSOR, split_axis=0, concat_axis=0, tiled=True)  5.91 us
    unnamed x17, local copies, waits for them, and re-layouts  3.58 us
  transfers between devices with their start and end apart: 5, of which 5 were waited for; matrix products, arithmetic and copies ran while one was open for 4% of the time, Pallas kernels for 0%

profile of v7, /device:TPU:6, one launch (start us, length us, event | category | flops | bytes accessed | tf_op | source)
XLA Modules:
  0.0 168.5 jit_solution(3450144224634961925)
XLA Ops:
  6.5 0.0 copy-start.2
  6.5 0.0 all-gather.5.cloned.1.call-start
  6.5 0.7 pad_clamp_fusion.1
  7.2 0.8 copy.61
  8.0 0.6 gather_fusion
  8.5 0.1 copy.62
  8.6 0.1 broadcast_in_dim.47
  8.7 0.1 and.45
  8.8 0.8 copy.63
  9.6 0.8 copy.64
  10.4 0.1 eq.38
  10.4 0.1 fusion.16
  10.6 0.2 reduce_window_sum.22
  10.8 0.2 select_reduce_fusion
  11.0 0.1 reduce_sum.24
  11.1 0.1 copy.68
  11.2 0.1 gather.13
  11.2 0.1 lt.87
  11.3 0.1 copy.77
  11.4 0.1 add.107
  11.5 0.1 copy.69
  11.6 0.2 fusion.14
  11.8 1.1 convolution_convert_fusion
  12.9 0.0 copy-start.4
  12.9 0.0 copy-start.5
  12.9 0.2 copy.70
  13.2 36.2 %all_to_all.15 = bf16[64,8,448]{2,1,0:T(8,128)(2,1)S(1)} all-to-all(bf16[64,8,448]{2,1,0:T(8,128)(2,1)S(1)} %bitcast.56), channel_id=1, replica_groups=mesh['expert'=64,'tx'=4,'tc'=2] {'expert'}, dimensions={0} | all-to-all | bytes 917504 | tf_op jit(solution)/shard_map/all_to_all | solution.py:70
  49.4 0.0 copy-done.2
  49.4 0.9 pad_maximum_fusion
  50.3 0.0 all-gather.5.cloned.1.call-update
  50.3 0.0 all-gather.7.cloned.1.call-start
  50.3 28.4 %all-gather.5.cloned.1.call-done = bf16[2176,448]{1,0:T(8,128)(2,1)} async-done(((bf16[544,448]{1,0:T(8,128)(2,1)}), bf16[2176,448]{1,0:T(8,128)(2,1)}) %all-gather.5.cloned.1.call-update) | async-done | bytes 1949712 | tf_op jit(solution)/shard_map/all_gather | solution.py:76
  78.8 1.9 %collective-permute-start = (bf16[4,544,448]{2,1,0:T(8,128)(2,1)}, bf16[4,544,448]{2,1,0:T(8,128)(2,1)}, u32[]{:S(2)}, u32[]{:S(2)}) collective-permute-start(bf16[4,544,448]{2,1,0:T(8,128)(2,1)} %bitcast.64), channel_id=1, source_target_pairs={{0,1},{1,0},{2,3},{3,2},{4,5},{5,4},{6,7},{7,6},{8,9},{9,8},{10,11... | collective-permute-start | bytes 5849096 | tf_op jit(solution)/shard_map/ppermute | solution.py:77
  80.7 0.0 copy-done.4
  80.7 0.0 copy-done.5
  80.7 2.4 %convolution_bitcast_fusion.2 = f32[544,256]{1,0:T(8,128)S(1)} fusion(bf16[4,544,448]{2,1,0:T(8,128)(2,1)} %bitcast.65, s32[]{:T(128)S(6)} %select_n.77, bf16[4,2,448,128]{3,2,1,0:T(8,128)(2,1)S(1)} %bitcast.68, bf16[4,2,448,128]{3,2,1,0:T(8,128)(2,1)S(1)} %bitcast.70), kind=kOutput, calls=%fused_computation.11 | convolution fusion | flops 500957184 | bytes 4341764 | tf_op jit(solution)/shard_map/xmc,xch->mh/dot_general | solution.py:82
  83.1 0.0 copy-start
  83.1 2.2 %collective-permute-done = bf16[4,544,448]{2,1,0:T(8,128)(2,1)} collective-permute-done((bf16[4,544,448]{2,1,0:T(8,128)(2,1)}, bf16[4,544,448]{2,1,0:T(8,128)(2,1)}, u32[]{:S(2)}, u32[]{:S(2)}) %collective-permute-start) | collective-permute-done | bytes 1949728 | tf_op jit(solution)/shard_map/ppermute | solution.py:77
  85.3 2.4 %multiply_convert_fusion = bf16[544,256]{1,0:T(8,128)(2,1)S(1)} fusion(f32[544,256]{1,0:T(8,128)S(1)} %convolution_bitcast_fusion.2, bf16[4,544,448]{2,1,0:T(8,128)(2,1)} %collective-permute-done, s32[]{:T(128)S(6)} %select_n.78, bf16[4,2,448,128]{3,2,1,0:T(8,128)(2,1)S(1)} %bitcast.69, bf16[4,2,448,128]{3,2,1,0:T(8,128)(2,1)S(1)} %bitcast.71), kind=kOutput, calls=%fused_computation.22 | convolution fusion | flops 501792768 | bytes 4620292 | tf_op jit(solution)/shard_map/xmc,xch->mh/dot_general | solution.py:84
  87.7 0.0 copy-start.1
  87.7 0.8 slice_select_fusion
  88.5 0.0 all-gather.7.cloned.1.call-update
  88.6 0.0 copy-done
  88.6 0.6 copy.73
  89.2 0.0 copy-done.1
  89.2 0.6 copy.74
  89.8 1.4 maximum_bitcast_fusion
  91.3 5.9 %all-to-all-start.1 = ((bf16[8,256,448]{1,2,0:T(8,128)(2,1)}), bf16[8,256,448]{1,2,0:T(8,128)(2,1)S(1)}, u32[]{:S(2)}, u32[]{:S(2)}) async-start(bf16[8,256,448]{1,2,0:T(8,128)(2,1)} %maximum_bitcast_fusion), calls=%async_computation.1 | async-start | bytes 3670016 | tf_op jit(solution)/shard_map/all_to_all | solution.py:64
  97.2 0.1 reduce_sum.23
  97.3 26.7 %all-to-all-done.1 = bf16[8,256,448]{1,2,0:T(8,128)(2,1)S(1)} async-done(((bf16[8,256,448]{1,2,0:T(8,128)(2,1)}), bf16[8,256,448]{1,2,0:T(8,128)(2,1)S(1)}, u32[]{:S(2)}, u32[]{:S(2)}) %all-to-all-start.1) | async-done | bytes 1835040 | tf_op jit(solution)/shard_map/all_to_all | solution.py:64
  123.9 1.6 all-gather.7.cloned.1.call-done
  125.5 1.9 %fusion = bf16[512,448]{0,1:T(8,128)(2,1)S(1)} fusion(bf16[8,544,128]{2,1,0:T(8,128)(2,1)} %bitcast.66, bf16[8,256,448]{1,2,0:T(8,128)(2,1)S(1)} %all-to-all-done.1), kind=kOutput, calls=%fused_computation.8 | convolution fusion | flops 469991424 | bytes 2424832 | tf_op jit(solution)/shard_map/imu,iuc->mc/dot_general | solution.py:89
  127.4 0.0 copy-start.3
  127.4 1.0 copy.75
  128.4 11.7 %all-to-all-start.2 = ((bf16[64,8,448]{2,1,0:T(8,128)(2,1)}), bf16[64,8,448]{2,1,0:T(8,128)(2,1)S(1)}, u32[]{:S(2)}, u32[]{:S(2)}) async-start(bf16[64,8,448]{2,1,0:T(8,128)(2,1)} %bitcast.17), calls=%async_computation.2 | async-start | bytes 1048576 | tf_op jit(solution)/shard_map/all_to_all | solution.py:101
  140.2 0.1 broadcast_compare_fusion
  140.2 0.1 reshape.226
  140.3 0.0 copy-done.3
  140.4 0.1 copy.76
  140.4 1.2 fusion.9
  141.7 17.9 %all-to-all-done.2 = bf16[64,8,448]{2,1,0:T(8,128)(2,1)S(1)} async-done(((bf16[64,8,448]{2,1,0:T(8,128)(2,1)}), bf16[64,8,448]{2,1,0:T(8,128)(2,1)S(1)}, u32[]{:S(2)}, u32[]{:S(2)}) %all-to-all-start.2) | async-done | bytes 458784 | tf_op jit(solution)/shard_map/all_to_all | solution.py:101
  159.5 1.2 gather_fusion.1
  160.7 0.3 multiply_reduce_fusion
  161.0 0.7 multiply_convert_fusion.1
  (11 shorter events, 0.1 us)
Async XLA Ops:
  6.5 42.9 %copy-start.2 = (bf16[2,16,448]{2,1,0:T(8,128)(2,1)S(1)}, bf16[2,16,448]{2,1,0:T(8,128)(2,1)}, u32[]{:S(2)}) copy-start(bf16[2,16,448]{2,1,0:T(8,128)(2,1)} %param.11) | copy-start | bytes 86020
  6.5 72.2 %all-gather.5.cloned.1.call-start = ((), (), s32[]{:S(2)}) async-start(), calls=%async_computation.3 | async-start | bytes 2785280 | tf_op jit(solution)/shard_map/all_gather | solution.py:76
  12.9 67.8 %copy-start.4 = (bf16[1,3584,128]{2,1,0:T(8,128)(2,1)S(1)}, bf16[1,3584,128]{2,1,0:T(8,128)(2,1)}, u32[]{:S(2)}) copy-start(bf16[1,3584,128]{2,1,0:T(8,128)(2,1)} %param.16) | copy-start | bytes 2752516
  12.9 67.8 %copy-start.5 = (bf16[3584,128]{1,0:T(8,128)(2,1)S(1)}, bf16[3584,128]{1,0:T(8,128)(2,1)}, u32[]{:S(2)}) copy-start(bf16[3584,128]{1,0:T(8,128)(2,1)} %param.18) | copy-start | bytes 2752516
  50.3 75.2 %all-gather.7.cloned.1.call-start = ((), (), s32[]{:S(2)}) async-start(), calls=%async_computation.4 | async-start | bytes 1253376 | tf_op jit(solution)/shard_map/all_gather | solution.py:88
  78.8 6.6 %collective-permute-start = (bf16[4,544,448]{2,1,0:T(8,128)(2,1)}, bf16[4,544,448]{2,1,0:T(8,128)(2,1)}, u32[]{:S(2)}, u32[]{:S(2)}) collective-permute-start(bf16[4,544,448]{2,1,0:T(8,128)(2,1)} %bitcast.64), channel_id=1, source_target_pairs={{0,1},{1,0},{2,3},{3,2},{4,5},{5,4},{6,7},{7,6},{8,9},{9,8},{10,11... | collective-permute-start | bytes 5849096 | tf_op jit(solution)/shard_map/ppermute | solution.py:77
  83.1 5.5 %copy-start = (bf16[1,128,3584]{2,1,0:T(8,128)(2,1)S(1)}, bf16[1,128,3584]{2,1,0:T(8,128)(2,1)}, u32[]{:S(2)}) copy-start(bf16[1,128,3584]{2,1,0:T(8,128)(2,1)} %param.17) | copy-start | bytes 2752516
  87.7 1.5 copy-start.1
  91.3 32.7 %all-to-all-start.1 = ((bf16[8,256,448]{1,2,0:T(8,128)(2,1)}), bf16[8,256,448]{1,2,0:T(8,128)(2,1)S(1)}, u32[]{:S(2)}, u32[]{:S(2)}) async-start(bf16[8,256,448]{1,2,0:T(8,128)(2,1)} %maximum_bitcast_fusion), calls=%async_computation.1 | async-start | bytes 3670016 | tf_op jit(solution)/shard_map/all_to_all | solution.py:64
  127.4 12.9 %copy-start.3 = (f32[2,16,8]{1,2,0:T(8,128)S(1)}, f32[2,16,8]{1,2,0:T(8,128)}, u32[]{:S(2)}) copy-start(f32[2,16,8]{1,2,0:T(8,128)} %param.15) | copy-start | bytes 3076
  128.4 31.1 %all-to-all-start.2 = ((bf16[64,8,448]{2,1,0:T(8,128)(2,1)}), bf16[64,8,448]{2,1,0:T(8,128)(2,1)S(1)}, u32[]{:S(2)}, u32[]{:S(2)}) async-start(bf16[64,8,448]{2,1,0:T(8,128)(2,1)} %bitcast.17), calls=%async_computation.2 | async-start | bytes 1048576 | tf_op jit(solution)/shard_map/all_to_all | solution.py:101
Sparse Core Ops, SparseCore 0:
  50.4 28.3 all-gather.4
  88.7 36.7 all-gather.6

commit v8 on v6

--- a/solution.py
+++ b/solution.py
@@ -56,8 +56,8 @@
     )
     hidden_units = slot_up.shape[2]
     down_parts = jnp.concatenate([slot_down[0], shared_down], axis=0)
-    down_parts = down_parts.reshape(-1, tensor_count, width_part).transpose(1, 0, 2)
-    down_cols = lax.all_to_all(down_parts, "tensor", split_axis=0, concat_axis=0, tiled=True)
+    down_cols = lax.all_to_all(down_parts, "tensor", split_axis=1, concat_axis=0, tiled=True)
+    down_cols = down_cols.reshape(tensor_count, -1, width_part)
     batch = jnp.dot(
         picker,
         hidden_rows.reshape(step_count * row_count, width_part),

time: 167 us -> 167 us (level)
  no operation moved by 1% of the time
where the time goes in v8:
time: 167 us; the launch traced here: 166 us
  waiting for transfers between devices  76 us (46%)
  blocking collectives  36.2 us (22%)
  starting transfers between devices  19.2 us (11%)
  between operations  13.6 us (8%)
  matrix products  7.74 us (5%)
  local copies, waits for them, and re-layouts  7.61 us (5%)
  other arithmetic  5.66 us (3%)
    all_to_all x1, blocking collectives, shards(): lax.all_to_all(batch, 'expert', split_axis=0, concat_axis=0, tiled=True)  36.2 us
    all_gather x1, waiting for transfers between devices, shards(): rows_all = lax.all_gather(rows_part, 'tensor', axis=0, tiled=False)  29.7 us
    all_to_all x1, waiting for transfers between devices, shards(): lax.all_to_all(down_parts, 'tensor', split_axis=1, concat_axis=0, tiled=T...  26.7 us
    all_to_all x1, waiting for transfers between devices, shards(): lax.all_to_all(routed_back, 'expert', split_axis=0, concat_axis=0, tiled=...  18.1 us
    all_to_all x1, starting transfers between devices, shards(): lax.all_to_all(routed_back, 'expert', split_axis=0, concat_axis=0, tiled=...  13.3 us
    all_to_all x1, starting transfers between devices, shards(): lax.all_to_all(down_parts, 'tensor', split_axis=1, concat_axis=0, tiled=T...  5.91 us
    unnamed x17, local copies, waits for them, and re-layouts  3.57 us
    dot_general x1, matrix products, shards(): jnp.einsum('tmc,tch->mh', rows_all, up_w, preferred_element_type=jnp.floa...  3.56 us
  transfers between devices with their start and end apart: 4, of which 4 were waited for; matrix products, arithmetic and copies ran while one was open for 3% of the time, Pallas kernels for 0%

profile of v8, /device:TPU:6, one launch (start us, length us, event | category | flops | bytes accessed | tf_op | source)
XLA Modules:
  0.0 166.1 jit_solution(7501884693797982086)
XLA Ops:
  6.5 0.0 copy-start.2
  6.5 0.0 all-gather.5.cloned.1.call-start
  6.5 0.7 pad_clamp_fusion.1
  7.2 0.8 copy.55
  8.0 0.6 gather_fusion
  8.5 0.1 copy.56
  8.6 0.1 broadcast_in_dim.47
  8.7 0.1 and.44
  8.8 0.8 copy.57
  9.6 0.8 copy.58
  10.4 0.1 eq.38
  10.4 0.1 fusion.16
  10.6 0.2 reduce_window_sum.22
  10.8 0.2 select_reduce_fusion
  11.0 0.1 reduce_sum.24
  11.1 0.1 copy.62
  11.2 0.1 gather.13
  11.2 0.1 lt.80
  11.3 0.1 copy.69
  11.4 0.1 add.96
  11.5 0.1 copy.63
  11.6 0.2 fusion.14
  11.8 1.1 convolution_convert_fusion
  12.9 0.0 copy-start.4
  12.9 0.2 copy.64
  13.1 0.0 copy-start.5
  13.2 36.2 %all_to_all.23 = bf16[64,8,448]{2,1,0:T(8,128)(2,1)S(1)} all-to-all(bf16[64,8,448]{2,1,0:T(8,128)(2,1)S(1)} %bitcast.38), channel_id=1, replica_groups=mesh['expert'=64,'tensor'=8] {'expert'}, dimensions={0} | all-to-all | bytes 917504 | tf_op jit(solution)/shard_map/all_to_all | solution.py:66
  49.4 0.0 copy-done.2
  49.4 0.9 pad_maximum_fusion.1
  50.3 0.0 all-gather.5.cloned.1.call-update
  50.3 0.0 all-gather.7.cloned.1.call-start
  50.3 29.7 %all-gather.5.cloned.1.call-done = bf16[4352,448]{1,0:T(8,128)(2,1)} async-done(((bf16[544,448]{1,0:T(8,128)(2,1)}), bf16[4352,448]{1,0:T(8,128)(2,1)}) %all-gather.5.cloned.1.call-update) | async-done | bytes 3899408 | tf_op jit(solution)/shard_map/all_gather | solution.py:72
  80.0 0.0 copy-done.4
  80.0 0.0 copy-done.5
  80.1 0.0 copy-start
  80.1 3.6 %multiply_convert_fusion = bf16[544,256]{1,0:T(8,128)(2,1)S(1)} fusion(bf16[8,544,448]{2,1,0:T(8,128)(2,1)} %bitcast.48, bf16[8,448,128]{2,1,0:T(8,128)(2,1)S(1)} %bitcast.51, bf16[8,448,128]{2,1,0:T(8,128)(2,1)S(1)} %bitcast.52), kind=kOutput, calls=%fused_computation.16 | convolution fusion | flops 1002610688 | bytes 6012928 | tf_op jit(solution)/shard_map/tmc,tch->mh/dot_general | solution.py:74
  83.6 0.0 copy-start.1
  83.6 0.8 slice_select_fusion
  84.4 0.0 all-gather.7.cloned.1.call-update
  84.5 0.0 copy-done
  84.5 0.6 copy.65
  85.1 0.0 copy-done.1
  85.1 0.6 copy.66
  85.7 1.4 pad_maximum_fusion
  87.2 5.9 %all-to-all-start.1 = ((bf16[256,8,448]{0,2,1:T(8,128)(2,1)}), bf16[256,8,448]{0,2,1:T(8,128)(2,1)S(1)}, u32[]{:S(2)}, u32[]{:S(2)}) async-start(bf16[256,8,448]{0,2,1:T(8,128)(2,1)} %pad_maximum_fusion), calls=%async_computation.1 | async-start | bytes 3670016 | tf_op jit(solution)/shard_map/all_to_all | solution.py:59
  93.1 0.1 reduce_sum.23
  93.2 26.7 %all-to-all-done.1 = bf16[256,8,448]{0,2,1:T(8,128)(2,1)S(1)} async-done(((bf16[256,8,448]{0,2,1:T(8,128)(2,1)}), bf16[256,8,448]{0,2,1:T(8,128)(2,1)S(1)}, u32[]{:S(2)}, u32[]{:S(2)}) %all-to-all-start.1) | async-done | bytes 1835040 | tf_op jit(solution)/shard_map/all_to_all | solution.py:59
  119.8 1.5 all-gather.7.cloned.1.call-done
  121.4 1.9 %fusion.4 = bf16[512,448]{0,1:T(8,128)(2,1)S(1)} fusion(bf16[8,544,128]{2,1,0:T(8,128)(2,1)} %bitcast.49, bf16[8,256,448]{1,2,0:T(8,128)(2,1)S(1)} %bitcast.40), kind=kOutput, calls=%fused_computation.8 | convolution fusion | flops 469991424 | bytes 2424832 | tf_op jit(solution)/shard_map/imu,iuc->mc/dot_general | solution.py:79
  123.3 0.0 copy-start.3
  123.3 1.0 copy.67
  124.3 13.3 %all-to-all-start.2 = ((bf16[64,8,448]{2,1,0:T(8,128)(2,1)}), bf16[64,8,448]{2,1,0:T(8,128)(2,1)S(1)}, u32[]{:S(2)}, u32[]{:S(2)}) async-start(bf16[64,8,448]{2,1,0:T(8,128)(2,1)} %bitcast.14), calls=%async_computation.2 | async-start | bytes 1048576 | tf_op jit(solution)/shard_map/all_to_all | solution.py:91
  137.6 0.1 broadcast_compare_fusion
  137.7 0.1 reshape.230
  137.8 0.0 copy-done.3
  137.8 0.1 copy.68
  137.9 1.2 fusion.9
  139.1 18.1 %all-to-all-done.2 = bf16[64,8,448]{2,1,0:T(8,128)(2,1)S(1)} async-done(((bf16[64,8,448]{2,1,0:T(8,128)(2,1)}), bf16[64,8,448]{2,1,0:T(8,128)(2,1)S(1)}, u32[]{:S(2)}, u32[]{:S(2)}) %all-to-all-start.2) | async-done | bytes 458784 | tf_op jit(solution)/shard_map/all_to_all | solution.py:91
  157.2 1.2 gather_fusion.1
  158.3 0.3 multiply_reduce_fusion
  158.6 0.7 multiply_convert_fusion.1
  (11 shorter events, 0.1 us)
Async XLA Ops:
  6.5 42.9 %copy-start.2 = (bf16[2,16,448]{2,1,0:T(8,128)(2,1)S(1)}, bf16[2,16,448]{2,1,0:T(8,128)(2,1)}, u32[]{:S(2)}) copy-start(bf16[2,16,448]{2,1,0:T(8,128)(2,1)} %param.11) | copy-start | bytes 86020
  6.5 73.5 %all-gather.5.cloned.1.call-start = ((), (), s32[]{:S(2)}) async-start(), calls=%async_computation.3 | async-start | bytes 5013504 | tf_op jit(solution)/shard_map/all_gather | solution.py:72
  12.9 67.1 %copy-start.4 = (bf16[3584,128]{1,0:T(8,128)(2,1)S(1)}, bf16[3584,128]{1,0:T(8,128)(2,1)}, u32[]{:S(2)}) copy-start(bf16[3584,128]{1,0:T(8,128)(2,1)} %param.18) | copy-start | bytes 2752516
  13.1 66.9 %copy-start.5 = (bf16[1,3584,128]{2,1,0:T(8,128)(2,1)S(1)}, bf16[1,3584,128]{2,1,0:T(8,128)(2,1)}, u32[]{:S(2)}) copy-start(bf16[1,3584,128]{2,1,0:T(8,128)(2,1)} %param.16) | copy-start | bytes 2752516
  50.3 71.1 %all-gather.7.cloned.1.call-start = ((), (), s32[]{:S(2)}) async-start(), calls=%async_computation.4 | async-start | bytes 1253376 | tf_op jit(solution)/shard_map/all_gather | solution.py:78
  80.1 4.4 %copy-start = (bf16[1,128,3584]{2,1,0:T(8,128)(2,1)S(1)}, bf16[1,128,3584]{2,1,0:T(8,128)(2,1)}, u32[]{:S(2)}) copy-start(bf16[1,128,3584]{2,1,0:T(8,128)(2,1)} %param.17) | copy-start | bytes 2752516
  83.6 1.5 copy-start.1
  87.2 32.7 %all-to-all-start.1 = ((bf16[256,8,448]{0,2,1:T(8,128)(2,1)}), bf16[256,8,448]{0,2,1:T(8,128)(2,1)S(1)}, u32[]{:S(2)}, u32[]{:S(2)}) async-start(bf16[256,8,448]{0,2,1:T(8,128)(2,1)} %pad_maximum_fusion), calls=%async_computation.1 | async-start | bytes 3670016 | tf_op jit(solution)/shard_map/all_to_all | solution.py:59
  123.3 14.5 %copy-start.3 = (f32[2,16,8]{1,2,0:T(8,128)S(1)}, f32[2,16,8]{1,2,0:T(8,128)}, u32[]{:S(2)}) copy-start(f32[2,16,8]{1,2,0:T(8,128)} %param.15) | copy-start | bytes 3076
  124.3 32.9 %all-to-all-start.2 = ((bf16[64,8,448]{2,1,0:T(8,128)(2,1)}), bf16[64,8,448]{2,1,0:T(8,128)(2,1)S(1)}, u32[]{:S(2)}, u32[]{:S(2)}) async-start(bf16[64,8,448]{2,1,0:T(8,128)(2,1)} %bitcast.14), calls=%async_computation.2 | async-start | bytes 1048576 | tf_op jit(solution)/shard_map/all_to_all | solution.py:91
Sparse Core Ops, SparseCore 0:
  50.4 29.5 all-gather.4
  84.6 36.7 all-gather.6

commit v9 on v8

--- a/solution.py
+++ b/solution.py
@@ -35,7 +35,7 @@
     return (live_mask, target, picker, weights)
 
 
-def shards(
+def layer(
     hidden_rows,
     draft_len,
     expert_ids,
@@ -71,6 +71,7 @@
     )
     rows_all = lax.all_gather(rows_part, "tensor", axis=0, tiled=False)
     up_w = jnp.concatenate([slot_up[0], shared_up], axis=1).reshape(tensor_count, width_part, -1)
+    up_w = lax.optimization_barrier(up_w)
     up_value = jnp.einsum("tmc,tch->mh", rows_all, up_w, preferred_element_type=jnp.float32)
     act = jax.nn.silu(up_value).astype(jnp.bfloat16)
     is_routed = (jnp.arange(served + own) < served)[:, None]
@@ -99,7 +100,7 @@
 
 def solution(mesh):
     return jax.shard_map(
-        shards,
+        layer,
         mesh=mesh,
         in_specs=(
             P(None, "expert", "tensor"),

time: 167 us -> 167 us (level)
  waiting for transfers between devices: 76 us -> 72.7 us
    all_gather x2, waiting for transfers between devices: 31.2 us -> 28.1 us  [the longest x1 28.1 us: layer(): rows_all = lax.all_gather(rows_part, 'tensor', axis=0, tiled=False)]
    concatenate x2 -> x3, other arithmetic: 2.31 us -> 3.9 us  [the longest x1 1.58 us: layer(): jnp.concatenate([slot_up[0], shared_up], axis=1)]
    unnamed x17 -> x13, local copies, waits for them, and re-layouts: 3.57 us -> 4.5 us
  transfers between devices with their start and end apart: 4 -> 4, of which waited for: 4 -> 3; matrix products, arithmetic and copies ran while one was open for 3% -> 4% of each run, Pallas kernels for 0% -> 0%
where the time goes in v9:
time: 167 us; the launch traced here: 165 us
  waiting for transfers between devices  72.7 us (44%)
  blocking collectives  36.2 us (22%)
  starting transfers between devices  19.2 us (11%)
  between operations  13.6 us (8%)
  local copies, waits for them, and re-layouts  8.54 us (5%)
  matrix products  7.64 us (5%)
  other arithmetic  7.24 us (4%)
    all_to_all x1, blocking collectives, layer(): lax.all_to_all(batch, 'expert', split_axis=0, concat_axis=0, tiled=True)  36.2 us
    all_gather x1, waiting for transfers between devices, layer(): rows_all = lax.all_gather(rows_part, 'tensor', axis=0, tiled=False)  28.1 us
    all_to_all x1, waiting for transfers between devices, layer(): lax.all_to_all(down_parts, 'tensor', split_axis=1, concat_axis=0, tiled=T...  26.7 us
    all_to_all x1, waiting for transfers between devices, layer(): lax.all_to_all(routed_back, 'expert', split_axis=0, concat_axis=0, tiled=...  17.9 us
    all_to_all x1, starting transfers between devices, layer(): lax.all_to_all(routed_back, 'expert', split_axis=0, concat_axis=0, tiled=...  13.3 us
    all_to_all x1, starting transfers between devices, layer(): lax.all_to_all(down_parts, 'tensor', split_axis=1, concat_axis=0, tiled=T...  5.91 us
    unnamed x13, local copies, waits for them, and re-layouts  4.5 us
    dot_general x1, matrix products, layer(): jnp.einsum('tmc,tch->mh', rows_all, up_w, preferred_element_type=jnp.floa...  3.46 us
  transfers between devices with their start and end apart: 4, of which 3 were waited for; matrix products, arithmetic and copies ran while one was open for 4% of the time, Pallas kernels for 0%

profile of v9, /device:TPU:6, one launch (start us, length us, event | category | flops | bytes accessed | tf_op | source)
XLA Modules:
  0.0 165.2 jit_solution(3185594459244773679)
XLA Ops:
  6.5 0.0 copy-start.2
  6.5 0.0 all-gather.5.cloned.1.call-start
  6.5 0.7 pad_clamp_fusion.1
  7.2 0.8 copy.55
  8.0 0.6 gather_fusion
  8.5 0.1 copy.56
  8.6 0.1 broadcast_in_dim.47
  8.7 0.1 and.44
  8.8 0.8 copy.57
  9.6 0.8 copy.58
  10.4 0.1 eq.38
  10.4 0.1 fusion.7
  10.6 0.2 reduce_window_sum.22
  10.8 0.2 select_reduce_fusion
  11.0 0.1 reduce_sum.24
  11.1 0.1 copy.62
  11.2 0.1 gather.13
  11.2 0.1 lt.80
  11.3 0.1 copy.69
  11.4 0.1 add.96
  11.5 0.1 copy.63
  11.6 0.2 fusion.5
  11.8 1.1 convolution_convert_fusion
  12.9 0.0 copy-start
  12.9 0.2 copy.64
  13.1 36.2 %all_to_all.23 = bf16[64,8,448]{2,1,0:T(8,128)(2,1)S(1)} all-to-all(bf16[64,8,448]{2,1,0:T(8,128)(2,1)S(1)} %bitcast.39), channel_id=1, replica_groups=mesh['expert'=64,'tensor'=8] {'expert'}, dimensions={0} | all-to-all | bytes 917504 | tf_op jit(solution)/shard_map/all_to_all | solution.py:66
  49.4 0.0 copy-done.2
  49.4 0.9 pad_maximum_fusion.2
  50.3 0.0 all-gather.5.cloned.1.call-update
  50.3 0.0 all-gather.7.cloned.1.call-start
  50.3 0.0 copy-done
  50.3 1.6 pad_maximum_fusion
  51.9 28.1 %all-gather.5.cloned.1.call-done = bf16[4352,448]{1,0:T(8,128)(2,1)} async-done(((bf16[544,448]{1,0:T(8,128)(2,1)}), bf16[4352,448]{1,0:T(8,128)(2,1)}) %all-gather.5.cloned.1.call-update) | async-done | bytes 3899408 | tf_op jit(solution)/shard_map/all_gather | solution.py:72
  80.0 3.5 %multiply_convert_fusion = bf16[544,256]{1,0:T(8,128)(2,1)S(1)} fusion(bf16[8,544,448]{2,1,0:T(8,128)(2,1)} %bitcast.51, bf16[8,448,256]{2,1,0:T(8,128)(2,1)S(1)} %pad_maximum_fusion), kind=kOutput, calls=%fused_computation.13 | convolution fusion | flops 998940672 | bytes 6012928 | tf_op jit(solution)/shard_map/tmc,tch->mh/dot_general | solution.py:75
  83.5 0.0 copy-start.1
  83.5 0.8 slice_select_fusion
  84.3 0.0 all-gather.7.cloned.1.call-update
  84.3 1.6 copy.65
  85.9 0.0 copy-done.1
  85.9 0.6 copy.66
  86.5 1.5 pad_maximum_fusion.1
  88.0 5.9 %all-to-all-start.1 = ((bf16[256,8,448]{0,2,1:T(8,128)(2,1)}), bf16[256,8,448]{0,2,1:T(8,128)(2,1)S(1)}, u32[]{:S(2)}, u32[]{:S(2)}) async-start(bf16[256,8,448]{0,2,1:T(8,128)(2,1)} %pad_maximum_fusion.1), calls=%async_computation.1 | async-start | bytes 3670016 | tf_op jit(solution)/shard_map/all_to_all | solution.py:59
  93.9 0.1 reduce_sum.23
  94.0 26.7 %all-to-all-done.1 = bf16[256,8,448]{0,2,1:T(8,128)(2,1)S(1)} async-done(((bf16[256,8,448]{0,2,1:T(8,128)(2,1)}), bf16[256,8,448]{0,2,1:T(8,128)(2,1)S(1)}, u32[]{:S(2)}, u32[]{:S(2)}) %all-to-all-start.1) | async-done | bytes 1835040 | tf_op jit(solution)/shard_map/all_to_all | solution.py:59
  120.7 0.0 all-gather.7.cloned.1.call-done
  120.7 1.9 %fusion = bf16[512,448]{0,1:T(8,128)(2,1)S(1)} fusion(bf16[8,544,128]{2,1,0:T(8,128)(2,1)} %bitcast.52, bf16[8,256,448]{1,2,0:T(8,128)(2,1)S(1)} %bitcast.41), kind=kOutput, calls=%fused_computation.5 | convolution fusion | flops 469991424 | bytes 2424832 | tf_op jit(solution)/shard_map/imu,iuc->mc/dot_general | solution.py:80
  122.6 0.0 copy-start.3
  122.6 1.0 copy.67
  123.6 13.3 %all-to-all-start.2 = ((bf16[64,8,448]{2,1,0:T(8,128)(2,1)}), bf16[64,8,448]{2,1,0:T(8,128)(2,1)S(1)}, u32[]{:S(2)}, u32[]{:S(2)}) async-start(bf16[64,8,448]{2,1,0:T(8,128)(2,1)} %bitcast.14), calls=%async_computation.2 | async-start | bytes 1048576 | tf_op jit(solution)/shard_map/all_to_all | solution.py:92
  136.9 0.1 broadcast_compare_fusion
  136.9 0.1 reshape.230
  137.0 0.0 copy-done.3
  137.1 0.1 copy.68
  137.1 1.2 fusion.2
  138.4 17.9 %all-to-all-done.2 = bf16[64,8,448]{2,1,0:T(8,128)(2,1)S(1)} async-done(((bf16[64,8,448]{2,1,0:T(8,128)(2,1)}), bf16[64,8,448]{2,1,0:T(8,128)(2,1)S(1)}, u32[]{:S(2)}, u32[]{:S(2)}) %all-to-all-start.2) | async-done | bytes 458784 | tf_op jit(solution)/shard_map/all_to_all | solution.py:92
  156.2 1.2 gather_fusion.1
  157.4 0.3 multiply_reduce_fusion
  157.7 0.7 multiply_convert_fusion.1
  (11 shorter events, 0.1 us)
Async XLA Ops:
  6.5 42.8 %copy-start.2 = (bf16[2,16,448]{2,1,0:T(8,128)(2,1)S(1)}, bf16[2,16,448]{2,1,0:T(8,128)(2,1)}, u32[]{:S(2)}) copy-start(bf16[2,16,448]{2,1,0:T(8,128)(2,1)} %param.11) | copy-start | bytes 86020
  6.5 73.5 %all-gather.5.cloned.1.call-start = ((), (), s32[]{:S(2)}) async-start(), calls=%async_computation.3 | async-start | bytes 5013504 | tf_op jit(solution)/shard_map/all_gather | solution.py:72
  12.9 37.4 %copy-start = (bf16[3584,128]{1,0:T(8,128)(2,1)S(1)}, bf16[3584,128]{1,0:T(8,128)(2,1)}, u32[]{:S(2)}) copy-start(bf16[3584,128]{1,0:T(8,128)(2,1)} %param.18) | copy-start | bytes 2752516
  50.3 70.4 %all-gather.7.cloned.1.call-start = ((), (), s32[]{:S(2)}) async-start(), calls=%async_computation.4 | async-start | bytes 1253376 | tf_op jit(solution)/shard_map/all_gather | solution.py:79
  83.5 2.4 %copy-start.1 = (bf16[128,3584]{1,0:T(8,128)(2,1)S(1)}, bf16[128,3584]{1,0:T(8,128)(2,1)}, u32[]{:S(2)}) copy-start(bf16[128,3584]{1,0:T(8,128)(2,1)} %param.19) | copy-start | bytes 2752516
  88.0 32.7 %all-to-all-start.1 = ((bf16[256,8,448]{0,2,1:T(8,128)(2,1)}), bf16[256,8,448]{0,2,1:T(8,128)(2,1)S(1)}, u32[]{:S(2)}, u32[]{:S(2)}) async-start(bf16[256,8,448]{0,2,1:T(8,128)(2,1)} %pad_maximum_fusion.1), calls=%async_computation.1 | async-start | bytes 3670016 | tf_op jit(solution)/shard_map/all_to_all | solution.py:59
  122.6 14.5 %copy-start.3 = (f32[2,16,8]{1,2,0:T(8,128)S(1)}, f32[2,16,8]{1,2,0:T(8,128)}, u32[]{:S(2)}) copy-start(f32[2,16,8]{1,2,0:T(8,128)} %param.15) | copy-start | bytes 3076
  123.6 32.7 %all-to-all-start.2 = ((bf16[64,8,448]{2,1,0:T(8,128)(2,1)}), bf16[64,8,448]{2,1,0:T(8,128)(2,1)S(1)}, u32[]{:S(2)}, u32[]{:S(2)}) async-start(bf16[64,8,448]{2,1,0:T(8,128)(2,1)} %bitcast.14), calls=%async_computation.2 | async-start | bytes 1048576 | tf_op jit(solution)/shard_map/all_to_all | solution.py:92
Sparse Core Ops, SparseCore 0:
  50.4 29.5 all-gather.4
  84.5 31.3 all-gather.6

commit v10 on v9

--- a/solution.py
+++ b/solution.py
@@ -66,16 +66,21 @@
     received = lax.all_to_all(batch, "expert", split_axis=0, concat_axis=0, tiled=True)
     served = received.shape[0] * received.shape[1]
     own = step_count * row_count
-    rows_part = jnp.concatenate(
-        [received.reshape(served, width_part), hidden_rows.reshape(own, width_part)], axis=0
+    served_all, own_all = lax.all_gather(
+        (received.reshape(served, width_part), hidden_rows.reshape(own, width_part)),
+        "tensor",
+        axis=0,
+        tiled=False,
     )
-    rows_all = lax.all_gather(rows_part, "tensor", axis=0, tiled=False)
-    up_w = jnp.concatenate([slot_up[0], shared_up], axis=1).reshape(tensor_count, width_part, -1)
-    up_w = lax.optimization_barrier(up_w)
-    up_value = jnp.einsum("tmc,tch->mh", rows_all, up_w, preferred_element_type=jnp.float32)
-    act = jax.nn.silu(up_value).astype(jnp.bfloat16)
-    is_routed = (jnp.arange(served + own) < served)[:, None]
-    act_own = jnp.where(is_routed, act[:, :hidden_units], act[:, hidden_units:])
+    up_w = slot_up[0].reshape(tensor_count, width_part, -1)
+    shared_w = shared_up.reshape(tensor_count, width_part, -1)
+    act_served = jax.nn.silu(
+        jnp.einsum("tmc,tch->mh", served_all, up_w, preferred_element_type=jnp.float32)
+    ).astype(jnp.bfloat16)
+    act_shared = jax.nn.silu(
+        jnp.einsum("tmc,tch->mh", own_all, shared_w, preferred_element_type=jnp.float32)
+    ).astype(jnp.bfloat16)
+    act_own = jnp.concatenate([act_served, act_shared], axis=0)
     act_all = lax.all_gather(act_own, "tensor", axis=0, tiled=False)
     routed_back = jnp.einsum(
         "imu,iuc->mc",

time: 167 us -> 164 us (0.982)
  waiting for transfers between devices: 72.7 us -> 57.9 us
  blocking collectives: 36.2 us -> 49.2 us
  other arithmetic: 7.24 us -> 4.72 us
    all_gather x1, waiting for transfers between devices: 28.1 us -> 13.3 us  [layer(): lax.all_gather((received.reshape(served, width_part), hidden_rows.reshape...]
    all_gather x0 -> x1, blocking collectives: none -> 13 us  [layer(): lax.all_gather((received.reshape(served, width_part), hidden_rows.reshape...]
    concatenate x2 -> x1, other arithmetic: 2.45 us -> 0.67 us  [layer(): act_own = jnp.concatenate([act_served, act_shared], axis=0)]
    dot_general x1 -> x2, matrix products: 3.46 us -> 3.62 us  [the longest x1 3.3 us: layer(): jnp.einsum('tmc,tch->mh', served_all, up_w, preferred_element_type=jnp.fl...]
    unnamed x13 -> x15, local copies, waits for them, and re-layouts: 4.5 us -> 4.51 us
  transfers between devices with their start and end apart: 4 -> 4, of which waited for: 3 -> 3; matrix products, arithmetic and copies ran while one was open for 4% -> 3% of each run, Pallas kernels for 0% -> 0%
where the time goes in v10:
time: 164 us; the launch traced here: 162 us
  waiting for transfers between devices  57.9 us (35%)
  blocking collectives  49.2 us (30%)
  starting transfers between devices  19.1 us (12%)
  between operations  13.6 us (8%)
  local copies, waits for them, and re-layouts  9.52 us (6%)
  matrix products  7.8 us (5%)
  other arithmetic  4.72 us (3%)
    all_to_all x1, blocking collectives, layer(): lax.all_to_all(batch, 'expert', split_axis=0, concat_axis=0, tiled=True)  36.2 us
    all_to_all x1, waiting for transfers between devices, layer(): lax.all_to_all(down_parts, 'tensor', split_axis=1, concat_axis=0, tiled=T...  26.7 us
    all_to_all x1, waiting for transfers between devices, layer(): lax.all_to_all(routed_back, 'expert', split_axis=0, concat_axis=0, tiled=...  17.9 us
    all_gather x1, waiting for transfers between devices, layer(): lax.all_gather((received.reshape(served, width_part), hidden_rows.reshape...  13.3 us
    all_to_all x1, starting transfers between devices, layer(): lax.all_to_all(routed_back, 'expert', split_axis=0, concat_axis=0, tiled=...  13.1 us
    all_gather x1, blocking collectives, layer(): lax.all_gather((received.reshape(served, width_part), hidden_rows.reshape...  13 us
    all_to_all x1, starting transfers between devices, layer(): lax.all_to_all(down_parts, 'tensor', split_axis=1, concat_axis=0, tiled=T...  5.9 us
    unnamed x15, local copies, waits for them, and re-layouts  4.51 us
  transfers between devices with their start and end apart: 4, of which 3 were waited for; matrix products, arithmetic and copies ran while one was open for 3% of the time, Pallas kernels for 0%

profile of v10, /device:TPU:6, one launch (start us, length us, event | category | flops | bytes accessed | tf_op | source)
XLA Modules:
  0.0 161.8 jit_solution(2600611236389828909)
XLA Ops:
  6.5 0.0 copy-start
  6.5 0.0 all-gather.4.cloned.1.call-start
  6.5 0.7 pad_clamp_fusion.1
  7.3 0.8 copy.74
  8.0 0.6 gather_fusion
  8.6 0.1 copy.75
  8.7 0.1 broadcast_in_dim.38
  8.8 0.1 and.44
  8.9 0.8 copy.76
  9.7 0.8 copy.77
  10.4 0.1 eq.38
  10.5 0.1 fusion.7
  10.7 0.2 reduce_window_sum.22
  10.9 0.2 select_reduce_fusion
  11.1 0.1 reduce_sum.24
  11.2 0.1 copy.81
  11.2 0.1 gather.13
  11.3 0.1 lt.68
  11.4 0.1 copy.89
  11.5 0.1 add.100
  11.6 0.1 copy.82
  11.7 0.2 fusion.5
  11.9 1.1 convolution_convert_fusion
  13.0 0.0 copy-start.3
  13.0 0.0 copy-start.2
  13.0 0.2 copy.83
  13.2 36.2 %all_to_all.23 = bf16[64,8,448]{2,1,0:T(8,128)(2,1)S(1)} all-to-all(bf16[64,8,448]{2,1,0:T(8,128)(2,1)S(1)} %bitcast.46), channel_id=1, replica_groups=mesh['expert'=64,'tensor'=8] {'expert'}, dimensions={0} | all-to-all | bytes 917504 | tf_op jit(solution)/shard_map/all_to_all | solution.py:66
  49.5 1.0 copy.84
  50.4 0.0 all-gather.4.cloned.1.call-update
  50.5 0.0 all-gather.6.cloned.1.call-start
  50.5 0.0 copy-done.3
  50.5 13.0 %all_gather.13 = bf16[8,32,448]{2,1,0:T(8,128)(2,1)S(1)} all-gather(bf16[1,32,448]{2,1,0:T(8,128)(2,1)S(1)} %bitcast.52), channel_id=1, replica_groups=mesh['expert'=64,'tensor'=8] {'tensor'}, dimensions={0}, use_global_device_ids=true | all-gather | bytes 258048 | tf_op jit(solution)/shard_map/all_gather | solution.py:69
  63.5 0.0 copy-done.2
  63.5 0.3 multiply_convert_fusion.2
  63.8 13.3 %all-gather.4.cloned.1.call-done = bf16[8,512,448]{1,2,0:T(8,128)(2,1)} async-done(((bf16[1,512,448]{1,2,0:T(8,128)(2,1)}), bf16[8,512,448]{1,2,0:T(8,128)(2,1)}) %all-gather.4.cloned.1.call-update) | async-done | bytes 3670032 | tf_op jit(solution)/shard_map/all_gather | solution.py:69
  77.1 0.0 copy-done
  77.1 0.0 copy-start.1
  77.1 3.3 %multiply_convert_fusion = bf16[512,128]{1,0:T(8,128)(2,1)S(1)} fusion(bf16[8,512,448]{1,2,0:T(8,128)(2,1)} %all-gather.4.cloned.1.call-done, bf16[8,448,128]{2,1,0:T(8,128)(2,1)S(1)} %bitcast.42), kind=kOutput, calls=%fused_computation.15 | convolution fusion | flops 470089728 | bytes 4718592 | tf_op jit(solution)/shard_map/tmc,tch->mh/dot_general | solution.py:78
  80.4 0.7 pad_maximum_fusion.1
  81.1 0.0 all-gather.6.cloned.1.call-update
  81.1 0.0 copy-done.1
  81.1 0.6 copy.85
  81.8 1.6 copy.86
  83.3 1.4 pad_maximum_fusion
  84.8 5.9 %all-to-all-start.1 = ((bf16[256,8,448]{0,2,1:T(8,128)(2,1)}), bf16[256,8,448]{0,2,1:T(8,128)(2,1)S(1)}, u32[]{:S(2)}, u32[]{:S(2)}) async-start(bf16[256,8,448]{0,2,1:T(8,128)(2,1)} %pad_maximum_fusion), calls=%async_computation.1 | async-start | bytes 3670016 | tf_op jit(solution)/shard_map/all_to_all | solution.py:59
  90.7 0.1 reduce_sum.23
  90.8 26.7 %all-to-all-done.1 = bf16[256,8,448]{0,2,1:T(8,128)(2,1)S(1)} async-done(((bf16[256,8,448]{0,2,1:T(8,128)(2,1)}), bf16[256,8,448]{0,2,1:T(8,128)(2,1)S(1)}, u32[]{:S(2)}, u32[]{:S(2)}) %all-to-all-start.1) | async-done | bytes 1835040 | tf_op jit(solution)/shard_map/all_to_all | solution.py:59
  117.4 0.0 all-gather.6.cloned.1.call-done
  117.4 1.9 %fusion = bf16[512,448]{0,1:T(8,128)(2,1)S(1)} fusion(bf16[8,544,128]{2,1,0:T(8,128)(2,1)} %bitcast.57, bf16[8,256,448]{1,2,0:T(8,128)(2,1)S(1)} %bitcast.48), kind=kOutput, calls=%fused_computation.4 | convolution fusion | flops 469991424 | bytes 2424832 | tf_op jit(solution)/shard_map/imu,iuc->mc/dot_general | solution.py:85
  119.3 0.0 copy-start.4
  119.4 1.0 copy.87
  120.4 13.1 %all-to-all-start.2 = ((bf16[64,8,448]{2,1,0:T(8,128)(2,1)}), bf16[64,8,448]{2,1,0:T(8,128)(2,1)S(1)}, u32[]{:S(2)}, u32[]{:S(2)}) async-start(bf16[64,8,448]{2,1,0:T(8,128)(2,1)} %bitcast.15), calls=%async_computation.2 | async-start | bytes 1048576 | tf_op jit(solution)/shard_map/all_to_all | solution.py:97
  133.5 0.1 broadcast_compare_fusion
  133.6 0.1 reshape.221
  133.6 0.0 copy-done.4
  133.7 0.1 copy.88
  133.8 1.2 fusion.2
  135.0 17.9 %all-to-all-done.2 = bf16[64,8,448]{2,1,0:T(8,128)(2,1)S(1)} async-done(((bf16[64,8,448]{2,1,0:T(8,128)(2,1)}), bf16[64,8,448]{2,1,0:T(8,128)(2,1)S(1)}, u32[]{:S(2)}, u32[]{:S(2)}) %all-to-all-start.2) | async-done | bytes 458784 | tf_op jit(solution)/shard_map/all_to_all | solution.py:97
  152.9 1.2 gather_fusion.1
  154.0 0.3 multiply_reduce_fusion
  154.3 0.7 multiply_convert_fusion.1
  (10 shorter events, 0.1 us)
Async XLA Ops:
  6.5 70.6 %copy-start = (bf16[1,3584,128]{2,1,0:T(8,128)(2,1)S(1)}, bf16[1,3584,128]{2,1,0:T(8,128)(2,1)}, u32[]{:S(2)}) copy-start(bf16[1,3584,128]{2,1,0:T(8,128)(2,1)} %param.16) | copy-start | bytes 2752516
  6.5 70.6 %all-gather.4.cloned.1.call-start = ((), (), s32[]{:S(2)}) async-start(), calls=%async_computation.3 | async-start | bytes 4128768 | tf_op jit(solution)/shard_map/all_gather | solution.py:69
  13.0 37.5 %copy-start.3 = (bf16[2,16,448]{2,1,0:T(8,128)(2,1)S(1)}, bf16[2,16,448]{2,1,0:T(8,128)(2,1)}, u32[]{:S(2)}) copy-start(bf16[2,16,448]{2,1,0:T(8,128)(2,1)} %param.11) | copy-start | bytes 86020
  13.0 50.5 %copy-start.2 = (bf16[3584,128]{1,0:T(8,128)(2,1)S(1)}, bf16[3584,128]{1,0:T(8,128)(2,1)}, u32[]{:S(2)}) copy-start(bf16[3584,128]{1,0:T(8,128)(2,1)} %param.18) | copy-start | bytes 2752516
  50.5 67.0 %all-gather.6.cloned.1.call-start = ((), (), s32[]{:S(2)}) async-start(), calls=%async_computation.4 | async-start | bytes 1253376 | tf_op jit(solution)/shard_map/all_gather | solution.py:84
  77.1 4.0 %copy-start.1 = (bf16[1,128,3584]{2,1,0:T(8,128)(2,1)S(1)}, bf16[1,128,3584]{2,1,0:T(8,128)(2,1)}, u32[]{:S(2)}) copy-start(bf16[1,128,3584]{2,1,0:T(8,128)(2,1)} %param.17) | copy-start | bytes 2752516
  84.8 32.7 %all-to-all-start.1 = ((bf16[256,8,448]{0,2,1:T(8,128)(2,1)}), bf16[256,8,448]{0,2,1:T(8,128)(2,1)S(1)}, u32[]{:S(2)}, u32[]{:S(2)}) async-start(bf16[256,8,448]{0,2,1:T(8,128)(2,1)} %pad_maximum_fusion), calls=%async_computation.1 | async-start | bytes 3670016 | tf_op jit(solution)/shard_map/all_to_all | solution.py:59
  119.3 14.3 %copy-start.4 = (f32[2,16,8]{1,2,0:T(8,128)S(1)}, f32[2,16,8]{1,2,0:T(8,128)}, u32[]{:S(2)}) copy-start(f32[2,16,8]{1,2,0:T(8,128)} %param.15) | copy-start | bytes 3076
  120.4 32.5 %all-to-all-start.2 = ((bf16[64,8,448]{2,1,0:T(8,128)(2,1)}), bf16[64,8,448]{2,1,0:T(8,128)(2,1)S(1)}, u32[]{:S(2)}, u32[]{:S(2)}) async-start(bf16[64,8,448]{2,1,0:T(8,128)(2,1)} %bitcast.15), calls=%async_computation.2 | async-start | bytes 1048576 | tf_op jit(solution)/shard_map/all_to_all | solution.py:97
Sparse Core Ops, SparseCore 0:
  50.6 26.5 all-gather.3
  81.3 31.0 all-gather.5

commit v11 on v10

--- a/solution.py
+++ b/solution.py
@@ -80,17 +80,18 @@
     act_shared = jax.nn.silu(
         jnp.einsum("tmc,tch->mh", own_all, shared_w, preferred_element_type=jnp.float32)
     ).astype(jnp.bfloat16)
-    act_own = jnp.concatenate([act_served, act_shared], axis=0)
-    act_all = lax.all_gather(act_own, "tensor", axis=0, tiled=False)
+    act_served_all, act_shared_all = lax.all_gather(
+        (act_served, act_shared), "tensor", axis=0, tiled=False
+    )
     routed_back = jnp.einsum(
         "imu,iuc->mc",
-        act_all[:, :served],
+        act_served_all,
         down_cols[:, :hidden_units],
         preferred_element_type=jnp.float32,
     ).astype(jnp.bfloat16).reshape(received.shape)
     shared_own = jnp.einsum(
         "imu,iuc->mc",
-        act_all[:, served:],
+        act_shared_all,
         down_cols[:, hidden_units:],
         preferred_element_type=jnp.float32,
     ).reshape(step_count, row_count, width_part)

time: 164 us -> 176 us (1.073)
  the two profiles are of different devices: /device:TPU:6 before, /device:TPU:1 now
where the time goes in v11:
time: 176 us; the launch traced here: 175 us
  blocking collectives  61.2 us (35%)
  waiting for transfers between devices  57.6 us (33%)
  starting transfers between devices  16.9 us (10%)
  between operations  13.6 us (8%)
  local copies, waits for them, and re-layouts  10.8 us (6%)
  matrix products  8.78 us (5%)
  other arithmetic  5.91 us (3%)
    all_to_all x1, blocking collectives, layer(): lax.all_to_all(batch, 'expert', split_axis=0, concat_axis=0, tiled=True)  34.3 us
    all_gather x1, waiting for transfers between devices, layer(): lax.all_gather((received.reshape(served, width_part), hidden_rows.reshape...  31.3 us
    all_to_all x1, waiting for transfers between devices, layer(): lax.all_to_all(down_parts, 'tensor', split_axis=1, concat_axis=0, tiled=T...  26.3 us
    all_gather x1, blocking collectives, layer(): lax.all_gather((received.reshape(served, width_part), hidden_rows.reshape...  14.1 us
    all_to_all x1, starting transfers between devices, layer(): lax.all_to_all(routed_back, 'expert', split_axis=0, concat_axis=0, tiled=...  13 us
    all_gather x1, blocking collectives, layer(): lax.all_gather((act_served, act_shared), 'tensor', axis=0, tiled=False)  12.8 us
    unnamed x19, local copies, waits for them, and re-layouts  4.51 us
    dot_general x1, matrix products, layer(): jnp.einsum('tmc,tch->mh', served_all, up_w, preferred_element_type=jnp.fl...  3.94 us
  transfers between devices with their start and end apart: 4, of which 2 were waited for; matrix products, arithmetic and copies ran while one was open for 5% of the time, Pallas kernels for 0%

profile of v11, /device:TPU:1, one launch (start us, length us, event | category | flops | bytes accessed | tf_op | source)
XLA Modules:
  0.0 174.9 jit_solution(1257247522296699674)
XLA Ops:
  6.5 0.0 copy-start
  6.5 0.0 all-gather.5.cloned.1.call-start
  6.5 0.7 pad_clamp_fusion.1
  7.3 0.8 copy.74
  8.0 0.6 gather_fusion
  8.6 0.1 copy.75
  8.7 0.1 broadcast_in_dim.38
  8.8 0.1 and.44
  8.9 0.8 copy.76
  9.7 0.8 copy.77
  10.4 0.1 eq.38
  10.5 0.1 fusion.6
  10.7 0.2 reduce_window_sum.22
  10.9 0.2 select_reduce_fusion
  11.1 0.1 reduce_sum.24
  11.2 0.1 copy.81
  11.2 0.1 gather.13
  11.3 0.1 lt.68
  11.4 0.1 copy.89
  11.5 0.1 add.100
  11.6 0.1 copy.82
  11.7 0.2 fusion.4
  11.9 1.1 convolution_convert_fusion
  13.0 0.2 copy.83
  13.2 34.3 %all_to_all.23 = bf16[64,8,448]{2,1,0:T(8,128)(2,1)S(1)} all-to-all(bf16[64,8,448]{2,1,0:T(8,128)(2,1)S(1)} %bitcast.52), channel_id=1, replica_groups=mesh['expert'=64,'tensor'=8] {'expert'}, dimensions={0} | all-to-all | bytes 917504 | tf_op jit(solution)/shard_map/all_to_all | solution.py:66
  47.6 1.0 copy.84
  48.5 0.0 all-gather.5.cloned.1.call-update
  48.5 0.0 all-gather.7.cloned.1.call-start
  48.6 31.3 %all-gather.5.cloned.1.call-done = bf16[8,512,448]{1,2,0:T(8,128)(2,1)} async-done(((bf16[1,512,448]{1,2,0:T(8,128)(2,1)}), bf16[8,512,448]{1,2,0:T(8,128)(2,1)}) %all-gather.5.cloned.1.call-update) | async-done | bytes 3670032 | tf_op jit(solution)/shard_map/all_gather | solution.py:69
  79.9 0.0 copy-done
  79.9 0.0 copy-start.1
  79.9 3.9 %multiply_convert_fusion = bf16[512,128]{1,0:T(8,128)(2,1)} fusion(bf16[8,512,448]{1,2,0:T(8,128)(2,1)} %all-gather.5.cloned.1.call-done, bf16[8,448,128]{2,1,0:T(8,128)(2,1)S(1)} %bitcast.45), kind=kOutput, calls=%fused_computation.14 | convolution fusion | flops 470089728 | bytes 4718592 | tf_op jit(solution)/shard_map/tmc,tch->mh/dot_general | solution.py:78
  83.9 0.0 all-gather.7.cloned.1.call-update
  83.9 0.0 copy-done.1
  83.9 0.6 copy.85
  84.5 1.6 copy.86
  86.1 1.4 pad_maximum_fusion
  87.5 0.0 copy-start.6
  87.5 3.9 %all-to-all-start.1 = ((bf16[256,8,448]{0,2,1:T(8,128)(2,1)}), bf16[256,8,448]{0,2,1:T(8,128)(2,1)S(1)}, u32[]{:S(2)}, u32[]{:S(2)}) async-start(bf16[256,8,448]{0,2,1:T(8,128)(2,1)} %pad_maximum_fusion), calls=%async_computation.1 | async-start | bytes 3670016 | tf_op jit(solution)/shard_map/all_to_all | solution.py:59
  91.4 0.1 reduce_sum.23
  91.5 0.0 copy-done.4
  91.5 0.0 copy-done.6
  91.5 0.6 broadcast_multiply_fusion.1
  92.1 0.7 broadcast_compare_fusion
  92.8 26.3 %all-to-all-done.1 = bf16[256,8,448]{0,2,1:T(8,128)(2,1)S(1)} async-done(((bf16[256,8,448]{0,2,1:T(8,128)(2,1)}), bf16[256,8,448]{0,2,1:T(8,128)(2,1)S(1)}, u32[]{:S(2)}, u32[]{:S(2)}) %all-to-all-start.1) | async-done | bytes 1835040 | tf_op jit(solution)/shard_map/all_to_all | solution.py:59
  119.1 1.9 %fusion = bf16[512,448]{0,1:T(8,128)(2,1)S(1)} fusion(bf16[8,512,128]{2,1,0:T(8,128)(2,1)} %bitcast.62, bf16[8,256,448]{1,2,0:T(8,128)(2,1)S(1)} %bitcast.47), kind=kOutput, calls=%fused_computation.4 | convolution fusion | flops 469991424 | bytes 2424832 | tf_op jit(solution)/shard_map/imu,iuc->mc/dot_general | solution.py:86
  121.0 0.0 copy-start.2
  121.0 1.0 copy.87
  122.0 13.0 %all-to-all-start.2 = ((bf16[64,8,448]{2,1,0:T(8,128)(2,1)}), bf16[64,8,448]{2,1,0:T(8,128)(2,1)S(1)}, u32[]{:S(2)}, u32[]{:S(2)}) async-start(bf16[64,8,448]{2,1,0:T(8,128)(2,1)} %bitcast.51), calls=%async_computation.2 | async-start | bytes 1048576 | tf_op jit(solution)/shard_map/all_to_all | solution.py:98
  135.0 14.1 %all_gather.21 = bf16[8,32,448]{2,1,0:T(8,128)(2,1)S(1)} all-gather(bf16[1,32,448]{2,1,0:T(8,128)(2,1)} %bitcast.58), channel_id=1, replica_groups=mesh['expert'=64,'tensor'=8] {'tensor'}, dimensions={0}, use_global_device_ids=true | all-gather | bytes 258048 | tf_op jit(solution)/shard_map/all_gather | solution.py:69
  149.1 0.0 copy-done.2
  149.1 0.7 reshape.220
  149.8 0.8 copy.88
  150.6 1.5 multiply_convert_fusion.2
  152.1 0.0 copy-start.3
  152.1 12.8 %all-gather.1 = bf16[256,128]{1,0:T(8,128)(2,1)S(1)} all-gather(bf16[32,128]{1,0:T(8,128)(2,1)S(1)} %multiply_convert_fusion.2), channel_id=3, replica_groups=mesh['expert'=64,'tensor'=8] {'tensor'}, dimensions={0}, use_global_device_ids=true | all-gather | bytes 73728 | tf_op jit(solution)/shard_map/all_gather | solution.py:83
  164.8 0.7 compare_select_fusion
  165.5 0.4 fusion.1
  165.9 0.0 all-to-all-done.2
  165.9 1.2 gather_fusion.1
  167.1 0.0 copy-done.3
  167.1 0.2 multiply_reduce_fusion
  167.3 0.0 copy-done.5
  167.4 0.7 multiply_convert_fusion.1
  (11 shorter events, 0.1 us)
Async XLA Ops:
  6.5 73.4 %copy-start = (bf16[1,3584,128]{2,1,0:T(8,128)(2,1)S(1)}, bf16[1,3584,128]{2,1,0:T(8,128)(2,1)}, u32[]{:S(2)}) copy-start(bf16[1,3584,128]{2,1,0:T(8,128)(2,1)} %param.16) | copy-start | bytes 2752516
  6.5 73.4 %all-gather.5.cloned.1.call-start = ((), (), s32[]{:S(2)}) async-start(), calls=%async_computation.3 | async-start | bytes 4128768 | tf_op jit(solution)/shard_map/all_gather | solution.py:69
  8.7 82.8 %copy-start.4 = (f32[2,16]{1,0:T(2,128)}, f32[2,16]{1,0:T(2,128)S(1)}, u32[]{:S(2)}) copy-start(f32[2,16]{1,0:T(2,128)S(1)} %get-tuple-element.21) | copy-start | bytes 388
  48.5 70.5 %all-gather.7.cloned.1.call-start = ((), (), s32[]{:S(2)}) async-start(), calls=%async_computation.4 | async-start | bytes 1179648 | tf_op jit(solution)/shard_map/all_gather | solution.py:83
  79.9 4.0 %copy-start.1 = (bf16[1,128,3584]{2,1,0:T(8,128)(2,1)S(1)}, bf16[1,128,3584]{2,1,0:T(8,128)(2,1)}, u32[]{:S(2)}) copy-start(bf16[1,128,3584]{2,1,0:T(8,128)(2,1)} %param.17) | copy-start | bytes 2752516
  87.5 4.0 %copy-start.6 = (f32[2,16,8]{1,2,0:T(8,128)S(1)}, f32[2,16,8]{1,2,0:T(8,128)}, u32[]{:S(2)}) copy-start(f32[2,16,8]{1,2,0:T(8,128)} %param.15) | copy-start | bytes 3076
  87.5 31.5 %all-to-all-start.1 = ((bf16[256,8,448]{0,2,1:T(8,128)(2,1)}), bf16[256,8,448]{0,2,1:T(8,128)(2,1)S(1)}, u32[]{:S(2)}, u32[]{:S(2)}) async-start(bf16[256,8,448]{0,2,1:T(8,128)(2,1)} %pad_maximum_fusion), calls=%async_computation.1 | async-start | bytes 3670016 | tf_op jit(solution)/shard_map/all_to_all | solution.py:59
  121.0 28.2 %copy-start.2 = (s32[2,16,8]{2,1,0:T(8,128)S(1)}, s32[2,16,8]{2,1,0:T(8,128)}, u32[]{:S(2)}) copy-start(s32[2,16,8]{2,1,0:T(8,128)} %get-tuple-element.20) | copy-start | bytes 3076
  122.0 43.9 %all-to-all-start.2 = ((bf16[64,8,448]{2,1,0:T(8,128)(2,1)}), bf16[64,8,448]{2,1,0:T(8,128)(2,1)S(1)}, u32[]{:S(2)}, u32[]{:S(2)}) async-start(bf16[64,8,448]{2,1,0:T(8,128)(2,1)} %bitcast.51), calls=%async_computation.2 | async-start | bytes 1048576 | tf_op jit(solution)/shard_map/all_to_all | solution.py:98
  152.1 15.0 %copy-start.3 = (pred[2,16,8]{2,1,0:T(8,128)(4,1)S(1)}, pred[2,16,8]{2,1,0:T(8,128)(4,1)}, u32[]{:S(2)}) copy-start(pred[2,16,8]{2,1,0:T(8,128)(4,1)} %get-tuple-element.19) | copy-start | bytes 772
  165.5 1.8 %copy-start.5 = (f32[2,16]{1,0:T(2,128)S(1)}, f32[2,16]{1,0:T(2,128)}, u32[]{:S(2)}) copy-start(f32[2,16]{1,0:T(2,128)} %copy-done.4) | copy-start | bytes 388
Sparse Core Ops, SparseCore 0:
  48.7 31.2 all-gather.4
  84.0 30.7 all-gather.6
